TPU v7x, 32 devices: a whole 2x2x4 slice. The times are simulated.
32 devices in a mesh: tensor: 2 (over y), req: 4 (over z), seq: 4 (over x, core).
Axes of the slice: x: 2, y: 2, z: 4, core: 2. Of those that a mesh axis runs over, the one named last changes fastest.
Arguments:
- draft_query: bfloat16 [4, 64, 8192], P('req', None, 'tensor'), may hold values from -6 to 6
- draft_kv: bfloat16 [4, 2, 64, 1024], P('req', None, None, 'tensor'), may hold values from -6 to 6
- own_cache: bfloat16 [4, 2, 32768, 1024], P('req', None, 'seq', 'tensor'), may hold values from -6 to 6
- shared_cache: bfloat16 [2, 2, 8192, 1024], P(None, None, ('req', 'seq'), 'tensor'), may hold values from -6 to 6
- out_weight: bfloat16 [8192, 8192], P(('tensor', 'seq')), may hold values from -0.09375 to 0.09375
- lengths: int32 [4], P('req'), may hold values from 1 to 32768, as said below
- group_ids: int32 [4], replicated, may hold values from 0 to 1
- parents: int32 [4, 64], P('req'), may hold values from -1 to 62, as said below
- accepted: int32 [4, 8], P('req'), may hold values from 0 to 62, as said below
Outputs:
- verified: bfloat16 [4, 64, 8192], P('req', None, ('tensor', 'seq'))
- accepted_kv: bfloat16 [4, 2, 8, 1024], P('req', None, None, 'tensor')
Inputs may be any that keep to these rules, and one draw needn't show every extreme that they name: Request r attends to own cache positions 0 to lengths[r] - 1; some request has exactly 32768. parents[r, 0] = -1 and 0 <= parents[r, i] < i for i >= 1. accepted[r, 0] = 0 and parents[r, accepted[r, a]] = accepted[r, a - 1]: a path from the root.
All inputs are finite; a program needn't handle non-finite values.
Results may differ from a plain program's by a relative error of at most 0.012.
Values may be sent and summed in bfloat16 or wider, within the bound.
No kernel may reach another device: no remote copies, remote signals or barrier semaphores. Data moves between devices by JAX's collectives and lax.ppermute only.
A program may use at most 192 MiB of HBM per device.

v0:
```python
import functools

import jax
import jax.numpy as jnp
from jax import lax
from jax.experimental import pallas as pl
from jax.experimental.pallas import tpu as pltpu
from jax.sharding import PartitionSpec as P


HD = 128
QPK = 8
NEG_FILL = -1e30
SCALE = HD ** (-0.5)
EXP2_SCALE = SCALE * 1.4426950408889634
OWN_BLOCK = 1024


def step(m_prev, l_prev, acc_prev, q, k, v, ones, ok):
    scores = lax.dot_general(
        q, k, (((1,), (1,)), ((), ())), preferred_element_type=jnp.float32
    )
    if ok is not None:
        scores = jnp.where(ok, scores, NEG_FILL)
    m_new = jnp.maximum(m_prev, jnp.max(scores, axis=1, keepdims=True))
    alpha = jnp.exp2((m_prev - m_new) * EXP2_SCALE)
    weights = jnp.exp2((scores - m_new) * EXP2_SCALE)
    if ok is not None:
        weights = jnp.where(ok, weights, 0.0)
    weights = weights.astype(jnp.bfloat16)
    l_new = alpha * l_prev + jnp.dot(weights, ones, preferred_element_type=jnp.float32)
    acc_new = alpha * acc_prev + jnp.dot(weights, v, preferred_element_type=jnp.float32)
    return m_new, l_new, acc_new


def own_kernel(kv_heads, block, nv_ref, q_ref, kv_ref, ones_ref, m_out, l_out, acc_out, m_s, l_s, acc_s):
    j = pl.program_id(0)
    n_valid = nv_ref[0]

    @pl.when(j == 0)
    def _():
        m_s[...] = jnp.full(m_s.shape, NEG_FILL, jnp.float32)
        l_s[...] = jnp.zeros(l_s.shape, jnp.float32)
        acc_s[...] = jnp.zeros(acc_s.shape, jnp.float32)

    start = j * block

    def body(masked):
        ok = None
        if masked:
            cols = start + lax.broadcasted_iota(jnp.int32, (1, block), 1)
            ok = cols < n_valid
        for h in range(kv_heads):
            cols_h = slice(h * HD, (h + 1) * HD)
            m, l, acc = step(
                m_s[h], l_s[h], acc_s[h], q_ref[h], kv_ref[0, :, cols_h], kv_ref[1, :, cols_h],
                ones_ref[...], ok,
            )
            m_s[h] = m
            l_s[h] = l
            acc_s[h] = acc

    full = start + block <= n_valid
    part = jnp.logical_and(start < n_valid, jnp.logical_not(full))
    pl.when(full)(lambda: body(False))
    pl.when(part)(lambda: body(True))

    @pl.when(j == pl.num_programs(0) - 1)
    def _():
        m_out[...] = m_s[...]
        l_out[...] = l_s[...]
        acc_out[...] = acc_s[...]


def own_attend(q, kv, n_valid):
    kv_heads, rows, _ = q.shape
    cache_len = kv.shape[1]
    block = min(OWN_BLOCK, cache_len)
    n_blocks = cache_len // block

    def kv_map(j, nv):
        last = jnp.maximum((nv[0] + block - 1) // block - 1, 0)
        return (0, jnp.minimum(j, last), 0)

    state_shapes = (
        jax.ShapeDtypeStruct((kv_heads, rows, 1), jnp.float32),
        jax.ShapeDtypeStruct((kv_heads, rows, HD), jnp.float32),
        jax.ShapeDtypeStruct((kv_heads, rows, HD), jnp.float32),
    )
    ones = jnp.ones((block, HD), jnp.bfloat16)
    full3 = lambda j, nv: (0, 0, 0)
    return pl.pallas_call(
        functools.partial(own_kernel, kv_heads, block),
        out_shape=state_shapes,
        grid_spec=pltpu.PrefetchScalarGridSpec(
            num_scalar_prefetch=1,
            grid=(n_blocks,),
            in_specs=[
                pl.BlockSpec(q.shape, full3),
                pl.BlockSpec((2, block, kv.shape[2]), kv_map),
                pl.BlockSpec(ones.shape, lambda j, nv: (0, 0)),
            ],
            out_specs=[pl.BlockSpec(s.shape, full3) for s in state_shapes],
            scratch_shapes=[pltpu.VMEM(s.shape, jnp.float32) for s in state_shapes],
        ),
        compiler_params=pltpu.CompilerParams(dimension_semantics=("arbitrary",)),
        cost_estimate=pl.CostEstimate(
            flops=6 * kv_heads * rows * cache_len * HD,
            transcendentals=kv_heads * rows * cache_len,
            bytes_accessed=kv.size * 2 + q.size * 2,
        ),
    )(n_valid, q, kv, ones)


def shared_kernel(kv_heads, n_blocks, with_tree, flag_ref, q_ref, m_ref, l_ref, acc_ref, *rest):
    blocks = rest[:n_blocks]
    ones_ref = rest[n_blocks]
    rest = rest[n_blocks + 1:]
    if with_tree:
        dkv_ref, reach_ref, tree_ones_ref = rest[:3]
        rest = rest[3:]
    m_out, l_out, acc_out = rest[:3]
    for h in range(kv_heads):
        cols_h = slice(h * HD, (h + 1) * HD)
        q = q_ref[h]
        m, l, acc = m_ref[h], l_ref[h], acc_ref[h]
        for blk in blocks:
            m, l, acc = step(
                m, l, acc, q, blk[0, :, cols_h], blk[1, :, cols_h], ones_ref[...], None
            )
        m_out[h] = m
        l_out[h] = l
        acc_out[h] = acc

    if with_tree:
        @pl.when(flag_ref[0] == 1)
        def _():
            ok = reach_ref[...] > 0.5
            for h in range(kv_heads):
                cols_h = slice(h * HD, (h + 1) * HD)
                m, l, acc = step(
                    m_out[h], l_out[h], acc_out[h], q_ref[h],
                    dkv_ref[0, :, cols_h], dkv_ref[1, :, cols_h], tree_ones_ref[...], ok,
                )
                m_out[h] = m
                l_out[h] = l
                acc_out[h] = acc


def shared_attend(q, state, blocks, tree=None):
    kv_heads, rows, _ = q.shape
    n_blocks = len(blocks)
    whole = lambda a: pl.BlockSpec(a.shape, lambda i, f: (0,) * a.ndim)
    ones = jnp.ones((blocks[0].shape[1], HD), jnp.bfloat16)
    operands = (q,) + tuple(state) + tuple(blocks) + (ones,)
    if tree is not None:
        draft_kv, reach_rows, flag = tree
        operands += (draft_kv, reach_rows, jnp.ones((draft_kv.shape[1], HD), jnp.bfloat16))
    else:
        flag = jnp.zeros((1,), jnp.int32)
    keys = sum(b.shape[1] for b in blocks)
    return pl.pallas_call(
        functools.partial(shared_kernel, kv_heads, n_blocks, tree is not None),
        out_shape=tuple(jax.ShapeDtypeStruct(s.shape, s.dtype) for s in state),
        grid_spec=pltpu.PrefetchScalarGridSpec(
            num_scalar_prefetch=1,
            grid=(1,),
            in_specs=[whole(a) for a in operands],
            out_specs=[whole(s) for s in state],
        ),
        compiler_params=pltpu.CompilerParams(vmem_limit_bytes=48 * 1024 * 1024),
        cost_estimate=pl.CostEstimate(
            flops=6 * kv_heads * rows * keys * HD,
            transcendentals=kv_heads * rows * keys,
            bytes_accessed=sum(b.size * 2 for b in blocks) + q.size * 2,
        ),
    )(flag, *operands)


def tree_reach(parent_row):
    node_count = parent_row.shape[0]
    nodes = jnp.arange(node_count, dtype=jnp.int32)
    reach = jnp.eye(node_count, dtype=jnp.float32) + (parent_row[:, None] == nodes[None, :]).astype(
        jnp.float32
    )
    for _ in range(max(node_count - 1, 1).bit_length()):
        reach = jnp.minimum(jnp.dot(reach, reach, precision=lax.Precision.HIGHEST), 1.0)
    return reach > 0.5


def pick_group(shared_cache, group_ids, request):
    onehot = jnp.arange(group_ids.shape[0], dtype=jnp.int32) == request
    group = jnp.sum(jnp.where(onehot, group_ids, 0))
    picked = shared_cache[:, 0]
    for g in range(1, shared_cache.shape[1]):
        picked = jnp.where(group == g, shared_cache[:, g], picked)
    return picked


def partner(index, k, count):
    if count & (count - 1) == 0:
        return index ^ k
    return (index + k) % count


def exchange_shared(shared_cache, group_ids, req_index, req_count, distances):
    received = [pick_group(shared_cache, group_ids, req_index)]
    for k in distances:
        pairs = [(r, partner(r, k, req_count)) for r in range(req_count)]
        sent = pick_group(shared_cache, group_ids, partner(req_index, k, req_count))
        received.append(lax.ppermute(sent, "req", pairs))
    return received


def exchange_to_owner(shared_cache, group_ids, req_index, seq_index, req_count, seq_count, k):
    picked = pick_group(shared_cache, group_ids, partner(req_index, k, req_count))
    received = []
    for d in range(seq_count):
        head = partner(seq_index, d, seq_count)
        piece = lax.dynamic_slice_in_dim(picked, head * HD, HD, 2)
        pairs = [
            (r * seq_count + q, partner(r, k, req_count) * seq_count + partner(q, d, seq_count))
            for r in range(req_count)
            for q in range(seq_count)
        ]
        received.append(lax.ppermute(piece, ("req", "seq"), pairs))
    return received


def split16(x):
    high = lax.reduce_precision(x, exponent_bits=8, mantissa_bits=7)
    low = (x - high).astype(jnp.bfloat16)
    return high.astype(jnp.bfloat16), low


def join16(high, low):
    return high.astype(jnp.float32) + low.astype(jnp.float32)


def layer(
    draft_query,
    draft_kv,
    own_cache,
    shared_cache,
    out_weight,
    lengths,
    group_ids,
    parents,
    accepted,
):
    kv_heads = own_cache.shape[3] // HD
    draft_len = draft_query.shape[1]
    rows = QPK * draft_len
    seq_count = lax.axis_size("seq")
    seq_index = lax.axis_index("seq")
    req_index = lax.axis_index("req")
    req_count = lax.axis_size("req")
    cache_len = own_cache.shape[2]

    distances = list(range(1, req_count))
    owner_mode = kv_heads == seq_count and len(distances) > 0
    if owner_mode:
        owner_blocks = exchange_to_owner(
            shared_cache, group_ids, req_index, seq_index, req_count, seq_count, distances[-1]
        )
        distances = distances[:-1]
    blocks = exchange_shared(shared_cache, group_ids, req_index, req_count, distances)

    queries = (
        draft_query[0]
        .reshape(draft_len, kv_heads, QPK, HD)
        .transpose(1, 2, 0, 3)
        .reshape(kv_heads, rows, HD)
    )
    n_valid = jnp.clip(lengths[0] - seq_index * cache_len, 0, cache_len).astype(jnp.int32)
    state = own_attend(queries, own_cache[0], n_valid.reshape(1))

    reach = tree_reach(parents[0])
    reach_rows = jnp.tile(reach.astype(jnp.float32), (QPK, 1))
    flag = (seq_index == 0).astype(jnp.int32).reshape(1)
    state = shared_attend(queries, state, blocks[:1], (draft_kv[0], reach_rows, flag))
    for blk in blocks[1:]:
        state = shared_attend(queries, state, [blk])
    m, l, acc = state

    heads_dev = kv_heads * QPK
    share = heads_dev // seq_count
    part_out = (acc / l).astype(jnp.bfloat16).reshape(heads_dev, draft_len, HD)
    m_hi, m_lo = split16(m[..., 0].reshape(heads_dev, draft_len))
    l_hi, l_lo = split16(l[..., 0].reshape(heads_dev, draft_len))
    stats = jnp.stack(
        [jnp.concatenate([m_hi, m_lo], 1), jnp.concatenate([l_hi, l_lo], 1)], 1
    )
    packed = jnp.concatenate([part_out, stats], 1)
    packed = lax.all_to_all(packed, "seq", 0, 0, tiled=True)
    packed = packed.reshape(seq_count, share, draft_len + 2, 2 * draft_len)
    part_max = join16(packed[:, :, draft_len, :draft_len], packed[:, :, draft_len, draft_len:])
    part_total = join16(
        packed[:, :, draft_len + 1, :draft_len], packed[:, :, draft_len + 1, draft_len:]
    )
    part_sum = packed[:, :, :draft_len, :].astype(jnp.float32)
    final_max = jnp.max(part_max, axis=0)
    factor = jnp.exp2((part_max - final_max[None]) * EXP2_SCALE) * part_total
    final_total = jnp.sum(factor, axis=0)
    final_sum = jnp.sum(part_sum * factor[..., None], axis=0)
    if owner_mode:
        rows_owned = share * draft_len
        owned_query = lax.dynamic_index_in_dim(queries, seq_index, 0, keepdims=True)
        owned_state = (
            final_max.reshape(1, rows_owned, 1),
            jnp.broadcast_to(final_total.reshape(1, rows_owned, 1), (1, rows_owned, HD)),
            final_sum.reshape(1, rows_owned, HD),
        )
        _, owned_total, owned_sum = shared_attend(owned_query, owned_state, owner_blocks)
        attended = (owned_sum / owned_total).reshape(share, draft_len, HD).astype(jnp.bfloat16)
    else:
        attended = (final_sum / final_total[..., None]).astype(jnp.bfloat16)
    attended = jnp.transpose(attended, (1, 0, 2)).reshape(draft_len, share * HD)
    out_group = ("tensor", "seq")
    owners = lax.axis_size("tensor") * seq_count
    columns = out_weight.shape[1] // owners
    product = jnp.einsum(
        "ik,kcj->cij",
        attended,
        out_weight.reshape(out_weight.shape[0], owners, columns),
        preferred_element_type=jnp.float32,
    ).astype(jnp.bfloat16)
    pieces = lax.all_to_all(product, out_group, 0, 0, tiled=True)
    verified = jnp.sum(pieces.astype(jnp.float32), axis=0).astype(jnp.bfloat16)[None]
    accepted_kv = jnp.take(draft_kv[0], accepted[0], axis=1)[None]
    return (verified, accepted_kv)


def solution(mesh):
    placed = (
        P("req", None, "tensor"),
        P("req", None, None, "tensor"),
        P("req", None, "seq", "tensor"),
        P(None, None, ("req", "seq"), "tensor"),
        P(("tensor", "seq"), None),
        P("req"),
        P(),
        P("req", None),
        P("req", None),
    )
    return jax.shard_map(
        layer,
        mesh=mesh,
        in_specs=placed,
        out_specs=(P("req", None, ("tensor", "seq")), P("req", None, None, "tensor")),
        check_vma=False,
    )
```

profile of v0, /device:TPU:8, one launch (start us, length us, event | category | flops | bytes accessed | tf_op | source)
XLA Modules:
  0.0 172.0 jit_solution(17883802221059353914)
XLA Ops:
  0.6 1.4 fusion.28
  4.6 0.0 copy-start.6
  4.6 3.5 %bitcast_select_fusion = (bf16[2,1,512,512]{3,2,0,1:T(8,128)(2,1)S(1)}, bf16[2,512,512]{2,1,0:T(8,128)(2,1)}, bf16[2,512,512]{2,1,0:T(8,128)(2,1)}, bf16[2,512,512]{2,1,0:T(8,128)(2,1)}) fusion(pred[]{:T(512)S(6)} %eq.74, bf16[2,2,512,512]{3,2,1,0:T(8,128)(2,1)} %param.12, pred[]{:T(512)S(6)} %eq.71, pred[]{:T(512)S(6)} %eq.68, pred[]{:T(512)S(6)} %eq.60), kind=kLoop, calls=%fused_computation.14 | loop fusion | flops 2097152 | bytes 6291460 | tf_op jit(solution)/shard_map/jit(_where)/select_n | solution.py:196
  8.1 0.0 collective-permute-start
  8.1 3.0 %collective-permute-start.1 = (bf16[2,512,512]{2,1,0:T(8,128)(2,1)}, bf16[2,512,512]{2,1,0:T(8,128)(2,1)S(1)}, u32[]{:S(2)}, u32[]{:S(2)}) collective-permute-start(bf16[2,512,512]{2,1,0:T(8,128)(2,1)} %get-tuple-element.39), channel_id=1, source_target_pairs={{0,8},{4,12},{8,0},{12,4},{1,9},{5,13},{9,1},{13,5},{2,10},{6,14},... | collective-permute-start | bytes 3145736 | tf_op jit(solution)/shard_map/ppermute | solution.py:211
  11.8 0.0 copy-done.6
  11.8 0.1 copy.35
  11.9 1.0 copy.18
  12.9 0.0 copy-done.7
  12.9 0.2 convolution_minimum_fusion.5
  13.1 0.2 convolution_minimum_fusion.4
  13.3 0.2 convolution_minimum_fusion.3
  13.5 0.2 convolution_minimum_fusion.2
  13.6 0.2 convolution_minimum_fusion.1
  13.8 0.2 fusion.10
  14.0 0.7 broadcast_in_dim.37.ones_ref
  14.7 21.6 %shard_map.104 = (f32[4,512,1]{2,1,0:T(8,128)}, f32[4,512,128]{2,1,0:T(8,128)}, f32[4,512,128]{2,1,0:T(8,128)}) custom-call(s32[1]{0:T(128)} %bitcast.5.nv_ref, bf16[4,512,128]{2,1,0:T(8,128)(2,1)} %bitcast.97, bf16[2,8192,512]{2,1,0:T(8,128)(2,1)} %bitcast.115, bf16[1024,128]{1,0:T(8,128)(2,1)} %broadcast_in_dim.37.ones_ref), custom_call_target="tpu_custom_call" | custom-call | flops 12884901888 | bytes 17301504 | tf_op jit(solution)/shard_map/pallas_call | solution.py:92
  36.3 0.0 copy-done
  36.4 1.2 copy-done.3
  37.6 6.9 %shard_map.105 = (f32[4,512,1]{2,1,0:T(8,128)S(1)}, f32[4,512,128]{2,1,0:T(8,128)S(1)}, f32[4,512,128]{2,1,0:T(8,128)S(1)}) custom-call(s32[1]{0:T(128)} %bitcast.3.flag_ref, bf16[4,512,128]{2,1,0:T(8,128)(2,1)S(1)} %bitcast.98, f32[4,512,1]{2,1,0:T(8,128)S(1)} %copy-done.3, f32[4,512,128]{2,1,0:T(8,128)} %get-tuple-element.17.l_ref, ...), custom_call_target="tpu_custom_call" | custom-call | flops 805306368 | bytes 1572864 | tf_op jit(solution)/shard_map/pallas_call | solution.py:162
  44.5 1.0 copy-done.1
  45.5 8.0 %collective-permute-done.rest_0_ = bf16[2,512,512]{2,1,0:T(8,128)(2,1)} collective-permute-done((bf16[2,512,512]{2,1,0:T(8,128)(2,1)}, bf16[2,512,512]{2,1,0:T(8,128)(2,1)}, u32[]{:S(2)}, u32[]{:S(2)}) %collective-permute-start) | collective-permute-done | bytes 1048608 | tf_op jit(solution)/shard_map/ppermute | solution.py:211
  53.4 4.8 %shard_map.106 = (f32[4,512,1]{2,1,0:T(8,128)S(1)}, f32[4,512,128]{2,1,0:T(8,128)S(1)}, f32[4,512,128]{2,1,0:T(8,128)S(1)}) custom-call(s32[1]{0:T(128)} %constant.17.clone.1.flag_ref, bf16[4,512,128]{2,1,0:T(8,128)(2,1)S(1)} %bitcast.99, f32[4,512,1]{2,1,0:T(8,128)S(1)} %get-tuple-element.19.m_ref, f32[4,512,128]{2,1,0:T(8,128)S(1)} %get-tuple-element.20.l_ref, ...), custom_call_target="tpu_custom_call" | custom-call | flops 805306368 | bytes 1572864 | tf_op jit(solution)/shard_map/pallas_call | solution.py:162
  58.3 1.0 copy-done.2
  59.3 0.0 collective-permute-done.1.rest_0_
  59.3 1.0 copy-done.5
  60.3 4.8 %shard_map.107 = (f32[4,512,1]{2,1,0:T(8,128)S(1)}, f32[4,512,128]{2,1,0:T(8,128)S(1)}, f32[4,512,128]{2,1,0:T(8,128)S(1)}) custom-call(s32[1]{0:T(128)} %constant.17.clone.1.flag_ref, bf16[4,512,128]{2,1,0:T(8,128)(2,1)S(1)} %bitcast.100, f32[4,512,1]{2,1,0:T(8,128)S(1)} %get-tuple-element.22.m_ref, f32[4,512,128]{2,1,0:T(8,128)S(1)} %get-tuple-element.23.l_ref, ...), custom_call_target="tpu_custom_call" | custom-call | flops 805306368 | bytes 1572864 | tf_op jit(solution)/shard_map/pallas_call | solution.py:162
  65.2 0.3 slice_reduce_fusion
  65.5 0.1 divide_convert_fusion
  65.7 0.3 reduce.2
  66.0 0.1 reshape_squeeze.10
  66.1 0.1 maximum_bitcast_fusion
  66.2 0.1 reshape_squeeze.11
  66.3 0.1 maximum_bitcast_fusion.1
  66.4 0.9 pad_maximum_fusion
  67.3 3.7 %all-to-all-start = ((bf16[32,66,128]{2,1,0:T(8,128)(2,1)}), bf16[32,66,128]{2,1,0:T(8,128)(2,1)S(1)}, u32[]{:S(2)}, u32[]{:S(2)}) async-start(bf16[32,66,128]{2,1,0:T(8,128)(2,1)} %pad_maximum_fusion), calls=%async_computation | async-start | bytes 1179648 | tf_op jit(solution)/shard_map/all_to_all | solution.py:295
  71.0 0.9 dynamic-slice_bitcast_fusion
  71.9 21.0 %collective-permute-start.2 = (bf16[2,512,128]{2,1,0:T(8,128)(2,1)}, bf16[2,512,128]{2,1,0:T(8,128)(2,1)S(1)}, u32[]{:S(2)}, u32[]{:S(2)}) collective-permute-start(bf16[2,512,128]{2,1,0:T(8,128)(2,1)} %get-tuple-element.45), channel_id=1, source_target_pairs={{0,12},{1,13},{2,14},{3,15},{4,8},{5,9},{6,10},{7,11},{8,4},{9,5},... | collective-permute-start | bytes 786440 | tf_op jit(solution)/shard_map/ppermute | solution.py:226
  92.9 0.0 collective-permute-start.3
  92.9 2.6 %collective-permute-start.4 = (bf16[2,512,128]{2,1,0:T(8,128)(2,1)S(1)}, bf16[2,512,128]{2,1,0:T(8,128)(2,1)S(1)}, u32[]{:S(2)}, u32[]{:S(2)}) collective-permute-start(bf16[2,512,128]{2,1,0:T(8,128)(2,1)S(1)} %get-tuple-element.43), channel_id=1, source_target_pairs={{0,14},{1,15},{2,12},{3,13},{4,10},{5,11},{6,8},{7,9},{8,6},{9,7},... | collective-permute-start | bytes 786440 | tf_op jit(solution)/shard_map/ppermute | solution.py:226
  95.6 0.3 collective-permute-start.5
  95.9 0.0 all-to-all-done
  95.9 0.1 fusion.32
  96.0 0.1 fusion.19
  96.1 0.2 reshape.151.m_ref
  96.3 0.1 broadcast_in_dim.40
  96.4 0.3 multiply_reduce_fusion
  96.7 25.5 %collective-permute-done.2.rest_0_ = bf16[2,512,128]{2,1,0:T(8,128)(2,1)S(1)} collective-permute-done((bf16[2,512,128]{2,1,0:T(8,128)(2,1)}, bf16[2,512,128]{2,1,0:T(8,128)(2,1)S(1)}, u32[]{:S(2)}, u32[]{:S(2)}) %collective-permute-start.2) | collective-permute-done | bytes 262176 | tf_op jit(solution)/shard_map/ppermute | solution.py:226
  122.2 5.5 %collective-permute-done.3.rest_1_ = bf16[2,512,128]{2,1,0:T(8,128)(2,1)S(1)} collective-permute-done((bf16[2,512,128]{2,1,0:T(8,128)(2,1)S(1)}, bf16[2,512,128]{2,1,0:T(8,128)(2,1)S(1)}, u32[]{:S(2)}, u32[]{:S(2)}) %collective-permute-start.3) | collective-permute-done | bytes 262176 | tf_op jit(solution)/shard_map/ppermute | solution.py:226
  127.7 6.5 %collective-permute-done.4.rest_2_ = bf16[2,512,128]{2,1,0:T(8,128)(2,1)S(1)} collective-permute-done((bf16[2,512,128]{2,1,0:T(8,128)(2,1)S(1)}, bf16[2,512,128]{2,1,0:T(8,128)(2,1)S(1)}, u32[]{:S(2)}, u32[]{:S(2)}) %collective-permute-start.4) | collective-permute-done | bytes 262176 | tf_op jit(solution)/shard_map/ppermute | solution.py:226
  134.2 5.5 %collective-permute-done.5.rest_3_ = bf16[2,512,128]{2,1,0:T(8,128)(2,1)S(1)} collective-permute-done((bf16[2,512,128]{2,1,0:T(8,128)(2,1)S(1)}, bf16[2,512,128]{2,1,0:T(8,128)(2,1)S(1)}, u32[]{:S(2)}, u32[]{:S(2)}) %collective-permute-start.5) | collective-permute-done | bytes 262176 | tf_op jit(solution)/shard_map/ppermute | solution.py:226
  139.7 0.1 broadcast_in_dim.41.l_ref
  139.9 3.6 %shard_map.108 = (f32[1,512,1]{2,1,0:T(8,128)}, f32[1,512,128]{2,1,0:T(8,128)S(1)}, f32[1,512,128]{2,1,0:T(8,128)S(1)}) custom-call(s32[1]{0:T(128)} %constant.17.clone.1.flag_ref, bf16[1,512,128]{2,1,0:T(8,128)(2,1)S(1)} %constant_dynamic-slice_fusion.q_ref, f32[1,512,1]{2,1,0:T(8,128)S(1)} %reshape.151.m_ref, f32[1,512,128]{2,1,0:T(8,128)S(1)} %broadcast_in_dim.41.l_ref, ...), custom_call_target="tpu_custom_call" | custom-call | flops 805306368 | bytes 1179648 | tf_op jit(solution)/shard_map/pallas_call | solution.py:162
  143.5 0.1 copy.26
  143.6 0.1 reshape.150
  143.7 8.4 %fusion.6 = bf16[8,64,1024]{2,1,0:T(8,128)(2,1)} fusion(bf16[64,1024,1]{1,0,2:T(8,128)(2,1)S(1)} %reshape.150, bf16[128,8,8,1024]{3,2,1,0:T(8,128)(2,1)} %bitcast.116), kind=kOutput, calls=%fused_computation.5 | convolution fusion | flops 1074266112 | bytes 17956864 | tf_op jit(solution)/shard_map/ik,kcj->cij/dot_general | solution.py:322
  152.1 3.7 %all-to-all-start.1 = ((bf16[8,64,1024]{2,1,0:T(8,128)(2,1)}), bf16[8,64,1024]{2,1,0:T(8,128)(2,1)S(1)}, u32[]{:S(2)}, u32[]{:S(2)}) async-start(bf16[8,64,1024]{2,1,0:T(8,128)(2,1)} %fusion.6), calls=%async_computation.1 | async-start | bytes 2097152 | tf_op jit(solution)/shard_map/all_to_all | solution.py:328
  155.8 0.1 copy.28
  155.9 0.0 copy-done.8
  156.0 0.6 gather_fusion
  156.6 0.1 broadcast_select_fusion
  156.7 0.6 copy.29
  157.3 13.8 %all-to-all-done.1 = bf16[8,64,1024]{2,1,0:T(8,128)(2,1)S(1)} async-done(((bf16[8,64,1024]{2,1,0:T(8,128)(2,1)}), bf16[8,64,1024]{2,1,0:T(8,128)(2,1)S(1)}, u32[]{:S(2)}, u32[]{:S(2)}) %all-to-all-start.1) | async-done | bytes 1048608 | tf_op jit(solution)/shard_map/all_to_all | solution.py:328
  171.1 0.8 reduce_sum.72
  (23 shorter events, 0.2 us)
Async XLA Ops:
  4.6 7.2 %copy-start.6 = (bf16[1,64,4096]{2,1,0:T(8,128)(2,1)S(1)}, bf16[1,64,4096]{2,1,0:T(8,128)(2,1)}, u32[]{:S(2)}) copy-start(bf16[1,64,4096]{2,1,0:T(8,128)(2,1)} %param.9) | copy-start | bytes 1572868
  8.1 4.8 %copy-start.7 = (s32[1,64]{1,0:T(1,128)S(1)}, s32[1,64]{1,0:T(1,128)}, u32[]{:S(2)}) copy-start(s32[1,64]{1,0:T(1,128)} %param.16) | copy-start | bytes 772
  8.1 45.4 %collective-permute-start = (bf16[2,512,512]{2,1,0:T(8,128)(2,1)}, bf16[2,512,512]{2,1,0:T(8,128)(2,1)}, u32[]{:S(2)}, u32[]{:S(2)}) collective-permute-start(bf16[2,512,512]{2,1,0:T(8,128)(2,1)} %get-tuple-element.40), channel_id=1, source_target_pairs={{0,4},{4,0},{8,12},{12,8},{1,5},{5,1},{9,13},{13,9},{2,6},{6,2},{1... | collective-permute-start | bytes 3145736 | tf_op jit(solution)/shard_map/ppermute | solution.py:211
  8.1 51.3 %collective-permute-start.1 = (bf16[2,512,512]{2,1,0:T(8,128)(2,1)}, bf16[2,512,512]{2,1,0:T(8,128)(2,1)S(1)}, u32[]{:S(2)}, u32[]{:S(2)}) collective-permute-start(bf16[2,512,512]{2,1,0:T(8,128)(2,1)} %get-tuple-element.39), channel_id=1, source_target_pairs={{0,8},{4,12},{8,0},{12,4},{1,9},{5,13},{9,1},{13,5},{2,10},{6,14},... | collective-permute-start | bytes 3145736 | tf_op jit(solution)/shard_map/ppermute | solution.py:211
  14.7 21.6 %copy-start = (bf16[64,4,8,128]{3,0,2,1:T(8,128)(2,1)S(1)}, bf16[64,4,8,128]{3,0,2,1:T(8,128)(2,1)}, u32[]{:S(2)}) copy-start(bf16[64,4,8,128]{3,0,2,1:T(8,128)(2,1)} %copy.18) | copy-start | bytes 1572868
  14.7 21.6 %copy-start.4 = (bf16[1,2,64,512]{3,2,1,0:T(8,128)(2,1)S(1)}, bf16[1,2,64,512]{3,2,1,0:T(8,128)(2,1)}, u32[]{:S(2)}) copy-start(bf16[1,2,64,512]{3,2,1,0:T(8,128)(2,1)} %param.10) | copy-start | bytes 393220
  36.3 1.2 copy-start.3
  44.5 1.0 copy-start.1
  58.3 1.0 copy-start.2
  59.3 1.0 copy-start.5
  67.3 28.6 %all-to-all-start = ((bf16[32,66,128]{2,1,0:T(8,128)(2,1)}), bf16[32,66,128]{2,1,0:T(8,128)(2,1)S(1)}, u32[]{:S(2)}, u32[]{:S(2)}) async-start(bf16[32,66,128]{2,1,0:T(8,128)(2,1)} %pad_maximum_fusion), calls=%async_computation | async-start | bytes 1179648 | tf_op jit(solution)/shard_map/all_to_all | solution.py:295
  71.9 50.3 %collective-permute-start.2 = (bf16[2,512,128]{2,1,0:T(8,128)(2,1)}, bf16[2,512,128]{2,1,0:T(8,128)(2,1)S(1)}, u32[]{:S(2)}, u32[]{:S(2)}) collective-permute-start(bf16[2,512,128]{2,1,0:T(8,128)(2,1)} %get-tuple-element.45), channel_id=1, source_target_pairs={{0,12},{1,13},{2,14},{3,15},{4,8},{5,9},{6,10},{7,11},{8,4},{9,5},... | collective-permute-start | bytes 786440 | tf_op jit(solution)/shard_map/ppermute | solution.py:226
  92.9 34.8 %collective-permute-start.3 = (bf16[2,512,128]{2,1,0:T(8,128)(2,1)S(1)}, bf16[2,512,128]{2,1,0:T(8,128)(2,1)S(1)}, u32[]{:S(2)}, u32[]{:S(2)}) collective-permute-start(bf16[2,512,128]{2,1,0:T(8,128)(2,1)S(1)} %get-tuple-element.44), channel_id=1, source_target_pairs={{0,13},{1,12},{2,15},{3,14},{4,9},{5,8},{6,11},{7,10},{8,5},{9,4},... | collective-permute-start | bytes 786440 | tf_op jit(solution)/shard_map/ppermute | solution.py:226
  92.9 41.3 %collective-permute-start.4 = (bf16[2,512,128]{2,1,0:T(8,128)(2,1)S(1)}, bf16[2,512,128]{2,1,0:T(8,128)(2,1)S(1)}, u32[]{:S(2)}, u32[]{:S(2)}) collective-permute-start(bf16[2,512,128]{2,1,0:T(8,128)(2,1)S(1)} %get-tuple-element.43), channel_id=1, source_target_pairs={{0,14},{1,15},{2,12},{3,13},{4,10},{5,11},{6,8},{7,9},{8,6},{9,7},... | collective-permute-start | bytes 786440 | tf_op jit(solution)/shard_map/ppermute | solution.py:226
  95.6 44.2 %collective-permute-start.5 = (bf16[2,512,128]{2,1,0:T(8,128)(2,1)S(1)}, bf16[2,512,128]{2,1,0:T(8,128)(2,1)S(1)}, u32[]{:S(2)}, u32[]{:S(2)}) collective-permute-start(bf16[2,512,128]{2,1,0:T(8,128)(2,1)S(1)} %get-tuple-element.42), channel_id=1, source_target_pairs={{0,15},{1,14},{2,13},{3,12},{4,11},{5,10},{6,9},{7,8},{8,7},{9,6},... | collective-permute-start | bytes 786440 | tf_op jit(solution)/shard_map/ppermute | solution.py:226
  152.1 3.8 %copy-start.8 = (s32[1,8]{1,0:T(1,128)S(1)}, s32[1,8]{1,0:T(1,128)}, u32[]{:S(2)}) copy-start(s32[1,8]{1,0:T(1,128)} %param.17) | copy-start | bytes 100
  152.1 19.0 %all-to-all-start.1 = ((bf16[8,64,1024]{2,1,0:T(8,128)(2,1)}), bf16[8,64,1024]{2,1,0:T(8,128)(2,1)S(1)}, u32[]{:S(2)}, u32[]{:S(2)}) async-start(bf16[8,64,1024]{2,1,0:T(8,128)(2,1)} %fusion.6), calls=%async_computation.1 | async-start | bytes 2097152 | tf_op jit(solution)/shard_map/all_to_all | solution.py:328
where the time goes:
time: 172 us
  waiting for transfers between devices  64.8 us (38%)
  Pallas kernels  41.8 us (24%)
  starting transfers between devices  34.4 us (20%)
  local copies, waits for them, and re-layouts  9.47 us (6%)
  matrix products  9.47 us (6%)
  other arithmetic  7.85 us (5%)
  between operations  4.2 us (2%)
    ppermute x4, waiting for transfers between devices, exchange_to_owner(): received.append(lax.ppermute(piece, ('req', 'seq'), pairs))  43 us
    ppermute x4, starting transfers between devices, exchange_to_owner(): received.append(lax.ppermute(piece, ('req', 'seq'), pairs))  24 us
    pallas_call x1, Pallas kernels, own_attend(): pl.pallas_call(functools.partial(own_kernel, kv_heads, block), out_shape=...  21.6 us
    pallas_call x4, Pallas kernels, shared_attend(): pl.pallas_call(functools.partial(shared_kernel, kv_heads, n_blocks, tree...  20.2 us
    all_to_all x1, waiting for transfers between devices, layer(): pieces = lax.all_to_all(product, out_group, 0, 0, tiled=True)  13.8 us
    dot_general x1, matrix products, layer(): jnp.einsum('ik,kcj->cij', attended, out_weight.reshape(out_weight.shape[0...  8.42 us
    ppermute x2, waiting for transfers between devices, exchange_shared(): received.append(lax.ppermute(sent, 'req', pairs))  7.99 us
    unnamed x20, local copies, waits for them, and re-layouts  4.9 us
  transfers between devices with their start and end apart: 8, of which 6 were waited for; matrix products, arithmetic and copies ran while one was open for 4% of the time, Pallas kernels for 19%

commit v1 on v0

--- a/solution.py
+++ b/solution.py
@@ -13,7 +13,7 @@
 NEG_FILL = -1e30
 SCALE = HD ** (-0.5)
 EXP2_SCALE = SCALE * 1.4426950408889634
-OWN_BLOCK = 1024
+OWN_BLOCK = 2048
 
 
 def step(m_prev, l_prev, acc_prev, q, k, v, ones, ok):
@@ -50,8 +50,9 @@
         if masked:
             cols = start + lax.broadcasted_iota(jnp.int32, (1, block), 1)
             ok = cols < n_valid
-        for h in range(kv_heads):
-            cols_h = slice(h * HD, (h + 1) * HD)
+
+        def head(h, carry):
+            cols_h = pl.ds(pl.multiple_of(h * HD, HD), HD)
             m, l, acc = step(
                 m_s[h], l_s[h], acc_s[h], q_ref[h], kv_ref[0, :, cols_h], kv_ref[1, :, cols_h],
                 ones_ref[...], ok,
@@ -59,6 +60,9 @@
             m_s[h] = m
             l_s[h] = l
             acc_s[h] = acc
+            return carry
+
+        lax.fori_loop(0, kv_heads, head, 0)
 
     full = start + block <= n_valid
     part = jnp.logical_and(start < n_valid, jnp.logical_not(full))
@@ -120,8 +124,9 @@
         dkv_ref, reach_ref, tree_ones_ref = rest[:3]
         rest = rest[3:]
     m_out, l_out, acc_out = rest[:3]
-    for h in range(kv_heads):
-        cols_h = slice(h * HD, (h + 1) * HD)
+
+    def head(h, carry):
+        cols_h = pl.ds(pl.multiple_of(h * HD, HD), HD)
         q = q_ref[h]
         m, l, acc = m_ref[h], l_ref[h], acc_ref[h]
         for blk in blocks:
@@ -131,6 +136,9 @@
         m_out[h] = m
         l_out[h] = l
         acc_out[h] = acc
+        return carry
+
+    lax.fori_loop(0, kv_heads, head, 0)
 
     if with_tree:
         @pl.when(flag_ref[0] == 1)
@@ -177,6 +185,30 @@
     )(flag, *operands)
 
 
+def project_kernel(a_ref, w_ref, o_ref):
+    o_ref[0] = jnp.dot(a_ref[...], w_ref[...], preferred_element_type=jnp.float32).astype(o_ref.dtype)
+
+
+def project(attended, out_weight, owners):
+    rows, depth = attended.shape
+    columns = out_weight.shape[1] // owners
+    return pl.pallas_call(
+        project_kernel,
+        out_shape=jax.ShapeDtypeStruct((owners, rows, columns), jnp.bfloat16),
+        grid=(owners,),
+        in_specs=[
+            pl.BlockSpec((rows, depth), lambda c: (0, 0)),
+            pl.BlockSpec((depth, columns), lambda c: (0, c)),
+        ],
+        out_specs=pl.BlockSpec((1, rows, columns), lambda c: (c, 0, 0)),
+        cost_estimate=pl.CostEstimate(
+            flops=2 * rows * depth * out_weight.shape[1],
+            transcendentals=0,
+            bytes_accessed=out_weight.size * 2 + attended.size * 2 + rows * out_weight.shape[1] * 2,
+        ),
+    )(attended, out_weight)
+
+
 def tree_reach(parent_row):
     node_count = parent_row.shape[0]
     nodes = jnp.arange(node_count, dtype=jnp.int32)
@@ -278,8 +310,8 @@
     reach = tree_reach(parents[0])
     reach_rows = jnp.tile(reach.astype(jnp.float32), (QPK, 1))
     flag = (seq_index == 0).astype(jnp.int32).reshape(1)
-    state = shared_attend(queries, state, blocks[:1], (draft_kv[0], reach_rows, flag))
-    for blk in blocks[1:]:
+    state = shared_attend(queries, state, blocks[:2], (draft_kv[0], reach_rows, flag))
+    for blk in blocks[2:]:
         state = shared_attend(queries, state, [blk])
     m, l, acc = state
 
@@ -318,13 +350,7 @@
     attended = jnp.transpose(attended, (1, 0, 2)).reshape(draft_len, share * HD)
     out_group = ("tensor", "seq")
     owners = lax.axis_size("tensor") * seq_count
-    columns = out_weight.shape[1] // owners
-    product = jnp.einsum(
-        "ik,kcj->cij",
-        attended,
-        out_weight.reshape(out_weight.shape[0], owners, columns),
-        preferred_element_type=jnp.float32,
-    ).astype(jnp.bfloat16)
+    product = project(attended, out_weight, owners)
     pieces = lax.all_to_all(product, out_group, 0, 0, tiled=True)
     verified = jnp.sum(pieces.astype(jnp.float32), axis=0).astype(jnp.bfloat16)[None]
     accepted_kv = jnp.take(draft_kv[0], accepted[0], axis=1)[None]

time: 172 us -> 168 us (0.977)
  starting transfers between devices: 34.4 us -> 18.9 us
  Pallas kernels: 41.8 us -> 55.5 us
  matrix products: 9.47 us -> 1.04 us
  waiting for transfers between devices: 64.8 us -> 70.8 us
    ppermute x4, starting transfers between devices: 24 us -> 8.54 us  [exchange_to_owner(): received.append(lax.ppermute(piece, ('req', 'seq'), pairs))]
    pallas_call x0 -> x1, Pallas kernels: none -> 10.3 us  [project(): pl.pallas_call(project_kernel, out_shape=jax.ShapeDtypeStruct((owners, ro...]
    dot_general x1 -> x0, matrix products: 8.42 us -> none  [layer(): jnp.einsum('ik,kcj->cij', attended, out_weight.reshape(out_weight.shape[0...]
    ppermute x2, waiting for transfers between devices: 7.99 us -> 14 us  [exchange_shared(): received.append(lax.ppermute(sent, 'req', pairs))]
    pallas_call x1, Pallas kernels: 21.6 us -> 24.6 us  [own_attend(): pl.pallas_call(functools.partial(own_kernel, kv_heads, block), out_shape=...]
    pallas_call x4 -> x3, Pallas kernels: 20.2 us -> 20.7 us  [shared_attend(): pl.pallas_call(functools.partial(shared_kernel, kv_heads, n_blocks, tree...]
    unnamed x20 -> x19, local copies, waits for them, and re-layouts: 4.9 us -> 4.63 us
  transfers between devices with their start and end apart: 8 -> 8, of which waited for: 6 -> 6; matrix products, arithmetic and copies ran while one was open for 4% -> 4% of each run, Pallas kernels for 19% -> 21%
where the time goes in v1:
time: 168 us
  waiting for transfers between devices  70.8 us (42%)
  Pallas kernels  55.5 us (33%)
  starting transfers between devices  18.9 us (11%)
  local copies, waits for them, and re-layouts  9.49 us (6%)
  other arithmetic  7.89 us (5%)
  between operations  4.16 us (2%)
    ppermute x4, waiting for transfers between devices, exchange_to_owner(): received.append(lax.ppermute(piece, ('req', 'seq'), pairs))  43 us
    pallas_call x1, Pallas kernels, own_attend(): pl.pallas_call(functools.partial(own_kernel, kv_heads, block), out_shape=...  24.6 us
    pallas_call x3, Pallas kernels, shared_attend(): pl.pallas_call(functools.partial(shared_kernel, kv_heads, n_blocks, tree...  20.7 us
    ppermute x2, waiting for transfers between devices, exchange_shared(): received.append(lax.ppermute(sent, 'req', pairs))  14 us
    all_to_all x1, waiting for transfers between devices, layer(): pieces = lax.all_to_all(product, out_group, 0, 0, tiled=True)  13.8 us
    pallas_call x1, Pallas kernels, project(): pl.pallas_call(project_kernel, out_shape=jax.ShapeDtypeStruct((owners, ro...  10.3 us
    ppermute x4, starting transfers between devices, exchange_to_owner(): received.append(lax.ppermute(piece, ('req', 'seq'), pairs))  8.54 us
    unnamed x19, local copies, waits for them, and re-layouts  4.63 us
  transfers between devices with their start and end apart: 8, of which 6 were waited for; matrix products, arithmetic and copies ran while one was open for 4% of the time, Pallas kernels for 21%

profile of v1, /device:TPU:8, one launch (start us, length us, event | category | flops | bytes accessed | tf_op | source)
XLA Modules:
  0.0 167.9 jit_solution(6078647321819216092)
XLA Ops:
  0.6 1.4 fusion.19
  4.6 0.0 copy-start.5
  4.6 3.5 %bitcast_select_fusion = (bf16[2,1,512,512]{3,2,0,1:T(8,128)(2,1)S(1)}, bf16[2,512,512]{2,1,0:T(8,128)(2,1)}, bf16[2,512,512]{2,1,0:T(8,128)(2,1)}, bf16[2,512,512]{2,1,0:T(8,128)(2,1)}) fusion(pred[]{:T(512)S(6)} %eq.74, bf16[2,2,512,512]{3,2,1,0:T(8,128)(2,1)} %param.12, pred[]{:T(512)S(6)} %eq.71, pred[]{:T(512)S(6)} %eq.63, pred[]{:T(512)S(6)} %eq.60), kind=kLoop, calls=%fused_computation.9 | loop fusion | flops 2097152 | bytes 6291460 | tf_op jit(solution)/shard_map/jit(_where)/select_n | solution.py:228
  8.1 0.0 collective-permute-start
  8.1 3.0 %collective-permute-start.1 = (bf16[2,512,512]{2,1,0:T(8,128)(2,1)}, bf16[2,512,512]{2,1,0:T(8,128)(2,1)S(1)}, u32[]{:S(2)}, u32[]{:S(2)}) collective-permute-start(bf16[2,512,512]{2,1,0:T(8,128)(2,1)} %get-tuple-element.33), channel_id=1, source_target_pairs={{0,8},{4,12},{8,0},{12,4},{1,9},{5,13},{9,1},{13,5},{2,10},{6,14},... | collective-permute-start | bytes 3145736 | tf_op jit(solution)/shard_map/ppermute | solution.py:243
  11.8 0.0 copy-done.5
  11.8 0.1 copy.32
  11.9 1.0 copy.17
  12.9 0.0 copy-done.6
  12.9 0.2 convolution_minimum_fusion.5
  13.1 0.2 convolution_minimum_fusion.4
  13.3 0.2 convolution_minimum_fusion.3
  13.5 0.2 convolution_minimum_fusion.2
  13.7 0.2 convolution_minimum_fusion.1
  13.8 0.2 fusion.1
  14.0 0.9 broadcast_in_dim.37.ones_ref
  14.9 24.6 %shard_map.104 = (f32[4,512,1]{2,1,0:T(8,128)}, f32[4,512,128]{2,1,0:T(8,128)}, f32[4,512,128]{2,1,0:T(8,128)}) custom-call(s32[1]{0:T(128)} %bitcast.5.nv_ref, bf16[4,512,128]{2,1,0:T(8,128)(2,1)} %bitcast.89, bf16[2,8192,512]{2,1,0:T(8,128)(2,1)} %bitcast.108, bf16[2048,128]{1,0:T(8,128)(2,1)} %broadcast_in_dim.37.ones_ref), custom_call_target="tpu_custom_call" | custom-call | flops 12884901888 | bytes 17301504 | tf_op jit(solution)/shard_map/pallas_call | solution.py:96
  39.5 14.0 %collective-permute-done.rest_1_ = bf16[2,512,512]{2,1,0:T(8,128)(2,1)} collective-permute-done((bf16[2,512,512]{2,1,0:T(8,128)(2,1)}, bf16[2,512,512]{2,1,0:T(8,128)(2,1)}, u32[]{:S(2)}, u32[]{:S(2)}) %collective-permute-start) | collective-permute-done | bytes 1048608 | tf_op jit(solution)/shard_map/ppermute | solution.py:243
  53.5 0.0 copy-done
  53.5 0.0 copy-done.3
  53.6 0.0 copy-start.1
  53.6 1.2 copy-done.1
  54.8 11.3 %shard_map.105 = (f32[4,512,1]{2,1,0:T(8,128)S(1)}, f32[4,512,128]{2,1,0:T(8,128)S(1)}, f32[4,512,128]{2,1,0:T(8,128)S(1)}) custom-call(s32[1]{0:T(128)} %bitcast.3.flag_ref, bf16[4,512,128]{2,1,0:T(8,128)(2,1)S(1)} %bitcast.90, f32[4,512,1]{2,1,0:T(8,128)S(1)} %copy-done.1, f32[4,512,128]{2,1,0:T(8,128)} %get-tuple-element.14.l_ref, ...), custom_call_target="tpu_custom_call" | custom-call | flops 1610612736 | bytes 2621440 | tf_op jit(solution)/shard_map/pallas_call | solution.py:170
  66.1 0.0 copy-start.2
  66.1 1.0 copy-done.2
  67.1 0.0 collective-permute-done.1.rest_0_
  67.1 1.0 copy-done.4
  68.1 5.7 %shard_map.106 = (f32[4,512,1]{2,1,0:T(8,128)S(1)}, f32[4,512,128]{2,1,0:T(8,128)S(1)}, f32[4,512,128]{2,1,0:T(8,128)S(1)}) custom-call(s32[1]{0:T(128)} %constant.17.clone.1.flag_ref, bf16[4,512,128]{2,1,0:T(8,128)(2,1)S(1)} %bitcast.91, f32[4,512,1]{2,1,0:T(8,128)S(1)} %get-tuple-element.16.m_ref, f32[4,512,128]{2,1,0:T(8,128)S(1)} %get-tuple-element.17.l_ref, ...), custom_call_target="tpu_custom_call" | custom-call | flops 805306368 | bytes 1572864 | tf_op jit(solution)/shard_map/pallas_call | solution.py:170
  73.9 0.3 slice_reduce_fusion
  74.2 0.1 divide_convert_fusion
  74.4 0.3 reduce.2
  74.7 0.1 reshape_squeeze.10
  74.8 0.1 maximum_bitcast_fusion
  74.9 0.1 reshape_squeeze.11
  75.0 0.1 maximum_bitcast_fusion.1
  75.1 0.9 pad_maximum_fusion
  76.0 3.7 %all-to-all-start = ((bf16[32,66,128]{2,1,0:T(8,128)(2,1)}), bf16[32,66,128]{2,1,0:T(8,128)(2,1)S(1)}, u32[]{:S(2)}, u32[]{:S(2)}) async-start(bf16[32,66,128]{2,1,0:T(8,128)(2,1)} %pad_maximum_fusion), calls=%async_computation | async-start | bytes 1179648 | tf_op jit(solution)/shard_map/all_to_all | solution.py:327
  79.7 1.1 dynamic-slice_bitcast_fusion
  80.8 5.6 %collective-permute-start.2 = (bf16[2,512,128]{2,1,0:T(8,128)(2,1)}, bf16[2,512,128]{2,1,0:T(8,128)(2,1)S(1)}, u32[]{:S(2)}, u32[]{:S(2)}) collective-permute-start(bf16[2,512,128]{2,1,0:T(8,128)(2,1)} %get-tuple-element.39), channel_id=1, source_target_pairs={{0,12},{1,13},{2,14},{3,15},{4,8},{5,9},{6,10},{7,11},{8,4},{9,5},... | collective-permute-start | bytes 786440 | tf_op jit(solution)/shard_map/ppermute | solution.py:258
  86.3 0.0 collective-permute-start.3
  86.4 2.7 %collective-permute-start.4 = (bf16[2,512,128]{2,1,0:T(8,128)(2,1)}, bf16[2,512,128]{2,1,0:T(8,128)(2,1)S(1)}, u32[]{:S(2)}, u32[]{:S(2)}) collective-permute-start(bf16[2,512,128]{2,1,0:T(8,128)(2,1)} %get-tuple-element.37), channel_id=1, source_target_pairs={{0,14},{1,15},{2,12},{3,13},{4,10},{5,11},{6,8},{7,9},{8,6},{9,7},... | collective-permute-start | bytes 786440 | tf_op jit(solution)/shard_map/ppermute | solution.py:258
  89.0 0.3 collective-permute-start.5
  89.3 0.0 all-to-all-done
  89.3 0.1 fusion.23
  89.4 0.1 fusion.10
  89.6 0.2 reshape.146.m_ref
  89.8 0.1 broadcast_in_dim.40
  89.8 0.3 multiply_reduce_fusion
  90.2 25.5 %collective-permute-done.2.rest_0_ = bf16[2,512,128]{2,1,0:T(8,128)(2,1)S(1)} collective-permute-done((bf16[2,512,128]{2,1,0:T(8,128)(2,1)}, bf16[2,512,128]{2,1,0:T(8,128)(2,1)S(1)}, u32[]{:S(2)}, u32[]{:S(2)}) %collective-permute-start.2) | collective-permute-done | bytes 262176 | tf_op jit(solution)/shard_map/ppermute | solution.py:258
  115.7 5.6 %collective-permute-done.3.rest_1_ = bf16[2,512,128]{2,1,0:T(8,128)(2,1)S(1)} collective-permute-done((bf16[2,512,128]{2,1,0:T(8,128)(2,1)}, bf16[2,512,128]{2,1,0:T(8,128)(2,1)S(1)}, u32[]{:S(2)}, u32[]{:S(2)}) %collective-permute-start.3) | collective-permute-done | bytes 262176 | tf_op jit(solution)/shard_map/ppermute | solution.py:258
  121.3 6.4 %collective-permute-done.4.rest_2_ = bf16[2,512,128]{2,1,0:T(8,128)(2,1)S(1)} collective-permute-done((bf16[2,512,128]{2,1,0:T(8,128)(2,1)}, bf16[2,512,128]{2,1,0:T(8,128)(2,1)S(1)}, u32[]{:S(2)}, u32[]{:S(2)}) %collective-permute-start.4) | collective-permute-done | bytes 262176 | tf_op jit(solution)/shard_map/ppermute | solution.py:258
  127.7 5.5 %collective-permute-done.5.rest_3_ = bf16[2,512,128]{2,1,0:T(8,128)(2,1)S(1)} collective-permute-done((bf16[2,512,128]{2,1,0:T(8,128)(2,1)}, bf16[2,512,128]{2,1,0:T(8,128)(2,1)S(1)}, u32[]{:S(2)}, u32[]{:S(2)}) %collective-permute-start.5) | collective-permute-done | bytes 262176 | tf_op jit(solution)/shard_map/ppermute | solution.py:258
  133.2 0.1 broadcast_in_dim.41.l_ref
  133.3 3.6 %shard_map.107 = (f32[1,512,1]{2,1,0:T(8,128)}, f32[1,512,128]{2,1,0:T(8,128)S(1)}, f32[1,512,128]{2,1,0:T(8,128)S(1)}) custom-call(s32[1]{0:T(128)} %constant.17.clone.1.flag_ref, bf16[1,512,128]{2,1,0:T(8,128)(2,1)S(1)} %constant_dynamic-slice_fusion.q_ref, f32[1,512,1]{2,1,0:T(8,128)S(1)} %reshape.146.m_ref, f32[1,512,128]{2,1,0:T(8,128)S(1)} %broadcast_in_dim.41.l_ref, ...), custom_call_target="tpu_custom_call" | custom-call | flops 805306368 | bytes 1179648 | tf_op jit(solution)/shard_map/pallas_call | solution.py:170
  137.0 0.1 copy.25
  137.1 0.7 copy.41
  137.7 10.3 %shard_map.108 = bf16[8,64,1024]{2,1,0:T(8,128)(2,1)} custom-call(bf16[64,1024]{1,0:T(8,128)(2,1)} %bitcast.102, bf16[1024,8192]{1,0:T(8,128)(2,1)} %w_ref.1), custom_call_target="tpu_custom_call" | custom-call | flops 1073741824 | bytes 17956864 | tf_op jit(solution)/shard_map/pallas_call | solution.py:195
  148.0 3.7 %all-to-all-start.1 = ((bf16[8,64,1024]{2,1,0:T(8,128)(2,1)}), bf16[8,64,1024]{2,1,0:T(8,128)(2,1)S(1)}, u32[]{:S(2)}, u32[]{:S(2)}) async-start(bf16[8,64,1024]{2,1,0:T(8,128)(2,1)} %shard_map.108), calls=%async_computation.1 | async-start | bytes 2097152 | tf_op jit(solution)/shard_map/all_to_all | solution.py:354
  151.7 0.1 copy.26
  151.9 0.6 gather_fusion
  152.5 0.1 broadcast_select_fusion
  152.6 0.6 copy.27
  153.2 13.8 %all-to-all-done.1 = bf16[8,64,1024]{2,1,0:T(8,128)(2,1)S(1)} async-done(((bf16[8,64,1024]{2,1,0:T(8,128)(2,1)}), bf16[8,64,1024]{2,1,0:T(8,128)(2,1)S(1)}, u32[]{:S(2)}, u32[]{:S(2)}) %all-to-all-start.1) | async-done | bytes 1048608 | tf_op jit(solution)/shard_map/all_to_all | solution.py:354
  167.0 0.8 reduce_sum.72
  (20 shorter events, 0.2 us)
Async XLA Ops:
  4.6 7.2 %copy-start.5 = (bf16[1,64,4096]{2,1,0:T(8,128)(2,1)S(1)}, bf16[1,64,4096]{2,1,0:T(8,128)(2,1)}, u32[]{:S(2)}) copy-start(bf16[1,64,4096]{2,1,0:T(8,128)(2,1)} %param.9) | copy-start | bytes 1572868
  8.1 4.8 %copy-start.6 = (s32[1,64]{1,0:T(1,128)S(1)}, s32[1,64]{1,0:T(1,128)}, u32[]{:S(2)}) copy-start(s32[1,64]{1,0:T(1,128)} %param.16) | copy-start | bytes 772
  8.1 45.4 %collective-permute-start = (bf16[2,512,512]{2,1,0:T(8,128)(2,1)}, bf16[2,512,512]{2,1,0:T(8,128)(2,1)}, u32[]{:S(2)}, u32[]{:S(2)}) collective-permute-start(bf16[2,512,512]{2,1,0:T(8,128)(2,1)} %get-tuple-element.34), channel_id=1, source_target_pairs={{0,4},{4,0},{8,12},{12,8},{1,5},{5,1},{9,13},{13,9},{2,6},{6,2},{1... | collective-permute-start | bytes 3145736 | tf_op jit(solution)/shard_map/ppermute | solution.py:243
  8.1 59.0 %collective-permute-start.1 = (bf16[2,512,512]{2,1,0:T(8,128)(2,1)}, bf16[2,512,512]{2,1,0:T(8,128)(2,1)S(1)}, u32[]{:S(2)}, u32[]{:S(2)}) collective-permute-start(bf16[2,512,512]{2,1,0:T(8,128)(2,1)} %get-tuple-element.33), channel_id=1, source_target_pairs={{0,8},{4,12},{8,0},{12,4},{1,9},{5,13},{9,1},{13,5},{2,10},{6,14},... | collective-permute-start | bytes 3145736 | tf_op jit(solution)/shard_map/ppermute | solution.py:243
  14.9 38.7 %copy-start = (bf16[64,4,8,128]{3,0,2,1:T(8,128)(2,1)S(1)}, bf16[64,4,8,128]{3,0,2,1:T(8,128)(2,1)}, u32[]{:S(2)}) copy-start(bf16[64,4,8,128]{3,0,2,1:T(8,128)(2,1)} %copy.17) | copy-start | bytes 1572868
  14.9 38.7 %copy-start.3 = (bf16[1,2,64,512]{3,2,1,0:T(8,128)(2,1)S(1)}, bf16[1,2,64,512]{3,2,1,0:T(8,128)(2,1)}, u32[]{:S(2)}) copy-start(bf16[1,2,64,512]{3,2,1,0:T(8,128)(2,1)} %param.10) | copy-start | bytes 393220
  53.6 1.2 copy-start.1
  66.1 1.0 copy-start.2
  67.1 1.0 copy-start.4
  76.0 13.3 %all-to-all-start = ((bf16[32,66,128]{2,1,0:T(8,128)(2,1)}), bf16[32,66,128]{2,1,0:T(8,128)(2,1)S(1)}, u32[]{:S(2)}, u32[]{:S(2)}) async-start(bf16[32,66,128]{2,1,0:T(8,128)(2,1)} %pad_maximum_fusion), calls=%async_computation | async-start | bytes 1179648 | tf_op jit(solution)/shard_map/all_to_all | solution.py:327
  80.8 34.9 %collective-permute-start.2 = (bf16[2,512,128]{2,1,0:T(8,128)(2,1)}, bf16[2,512,128]{2,1,0:T(8,128)(2,1)S(1)}, u32[]{:S(2)}, u32[]{:S(2)}) collective-permute-start(bf16[2,512,128]{2,1,0:T(8,128)(2,1)} %get-tuple-element.39), channel_id=1, source_target_pairs={{0,12},{1,13},{2,14},{3,15},{4,8},{5,9},{6,10},{7,11},{8,4},{9,5},... | collective-permute-start | bytes 786440 | tf_op jit(solution)/shard_map/ppermute | solution.py:258
  86.3 35.0 %collective-permute-start.3 = (bf16[2,512,128]{2,1,0:T(8,128)(2,1)}, bf16[2,512,128]{2,1,0:T(8,128)(2,1)S(1)}, u32[]{:S(2)}, u32[]{:S(2)}) collective-permute-start(bf16[2,512,128]{2,1,0:T(8,128)(2,1)} %get-tuple-element.38), channel_id=1, source_target_pairs={{0,13},{1,12},{2,15},{3,14},{4,9},{5,8},{6,11},{7,10},{8,5},{9,4},... | collective-permute-start | bytes 786440 | tf_op jit(solution)/shard_map/ppermute | solution.py:258
  86.4 41.3 %collective-permute-start.4 = (bf16[2,512,128]{2,1,0:T(8,128)(2,1)}, bf16[2,512,128]{2,1,0:T(8,128)(2,1)S(1)}, u32[]{:S(2)}, u32[]{:S(2)}) collective-permute-start(bf16[2,512,128]{2,1,0:T(8,128)(2,1)} %get-tuple-element.37), channel_id=1, source_target_pairs={{0,14},{1,15},{2,12},{3,13},{4,10},{5,11},{6,8},{7,9},{8,6},{9,7},... | collective-permute-start | bytes 786440 | tf_op jit(solution)/shard_map/ppermute | solution.py:258
  89.0 44.2 %collective-permute-start.5 = (bf16[2,512,128]{2,1,0:T(8,128)(2,1)}, bf16[2,512,128]{2,1,0:T(8,128)(2,1)S(1)}, u32[]{:S(2)}, u32[]{:S(2)}) collective-permute-start(bf16[2,512,128]{2,1,0:T(8,128)(2,1)} %get-tuple-element.36), channel_id=1, source_target_pairs={{0,15},{1,14},{2,13},{3,12},{4,11},{5,10},{6,9},{7,8},{8,7},{9,6},... | collective-permute-start | bytes 786440 | tf_op jit(solution)/shard_map/ppermute | solution.py:258
  148.0 3.8 %copy-start.7 = (s32[1,8]{1,0:T(1,128)S(1)}, s32[1,8]{1,0:T(1,128)}, u32[]{:S(2)}) copy-start(s32[1,8]{1,0:T(1,128)} %param.17) | copy-start | bytes 100
  148.0 19.0 %all-to-all-start.1 = ((bf16[8,64,1024]{2,1,0:T(8,128)(2,1)}), bf16[8,64,1024]{2,1,0:T(8,128)(2,1)S(1)}, u32[]{:S(2)}, u32[]{:S(2)}) async-start(bf16[8,64,1024]{2,1,0:T(8,128)(2,1)} %shard_map.108), calls=%async_computation.1 | async-start | bytes 2097152 | tf_op jit(solution)/shard_map/all_to_all | solution.py:354

commit v2 on v1

--- a/solution.py
+++ b/solution.py
@@ -185,30 +185,6 @@
     )(flag, *operands)
 
 
-def project_kernel(a_ref, w_ref, o_ref):
-    o_ref[0] = jnp.dot(a_ref[...], w_ref[...], preferred_element_type=jnp.float32).astype(o_ref.dtype)
-
-
-def project(attended, out_weight, owners):
-    rows, depth = attended.shape
-    columns = out_weight.shape[1] // owners
-    return pl.pallas_call(
-        project_kernel,
-        out_shape=jax.ShapeDtypeStruct((owners, rows, columns), jnp.bfloat16),
-        grid=(owners,),
-        in_specs=[
-            pl.BlockSpec((rows, depth), lambda c: (0, 0)),
-            pl.BlockSpec((depth, columns), lambda c: (0, c)),
-        ],
-        out_specs=pl.BlockSpec((1, rows, columns), lambda c: (c, 0, 0)),
-        cost_estimate=pl.CostEstimate(
-            flops=2 * rows * depth * out_weight.shape[1],
-            transcendentals=0,
-            bytes_accessed=out_weight.size * 2 + attended.size * 2 + rows * out_weight.shape[1] * 2,
-        ),
-    )(attended, out_weight)
-
-
 def tree_reach(parent_row):
     node_count = parent_row.shape[0]
     nodes = jnp.arange(node_count, dtype=jnp.int32)
@@ -350,9 +326,20 @@
     attended = jnp.transpose(attended, (1, 0, 2)).reshape(draft_len, share * HD)
     out_group = ("tensor", "seq")
     owners = lax.axis_size("tensor") * seq_count
-    product = project(attended, out_weight, owners)
-    pieces = lax.all_to_all(product, out_group, 0, 0, tiled=True)
-    verified = jnp.sum(pieces.astype(jnp.float32), axis=0).astype(jnp.bfloat16)[None]
+    columns = out_weight.shape[1] // owners
+    blocked = out_weight.reshape(out_weight.shape[0], owners, columns)
+    half = columns // 2
+    halves = []
+    for lo in (0, half):
+        product = jnp.einsum(
+            "ik,kcj->cij",
+            attended,
+            blocked[:, :, lo:lo + half],
+            preferred_element_type=jnp.float32,
+        ).astype(jnp.bfloat16)
+        pieces = lax.all_to_all(product, out_group, 0, 0, tiled=True)
+        halves.append(jnp.sum(pieces.astype(jnp.float32), axis=0).astype(jnp.bfloat16))
+    verified = jnp.concatenate(halves, 1)[None]
     accepted_kv = jnp.take(draft_kv[0], accepted[0], axis=1)[None]
     return (verified, accepted_kv)
 

time: 168 us -> 173 us (1.030)
  waiting for transfers between devices: 70.8 us -> 44.4 us
  local copies, waits for them, and re-layouts: 9.49 us -> 32.2 us
  matrix products: 1.04 us -> 14.7 us
  Pallas kernels: 55.5 us -> 45.3 us
  starting transfers between devices: 18.9 us -> 23.3 us
    unnamed x19 -> x17, local copies, waits for them, and re-layouts: 4.63 us -> 27.4 us
    ppermute x4, waiting for transfers between devices: 43 us -> 20.5 us  [exchange_to_owner(): received.append(lax.ppermute(piece, ('req', 'seq'), pairs))]
    dot_general x0 -> x2, matrix products: none -> 13.7 us  [layer(): jnp.einsum('ik,kcj->cij', attended, blocked[:, :, lo:lo + half], preferre...]
    pallas_call x1 -> x0, Pallas kernels: 10.3 us -> none  [project(): pl.pallas_call(project_kernel, out_shape=jax.ShapeDtypeStruct((owners, ro...]
    all_to_all x1 -> x2, starting transfers between devices: 3.69 us -> 6.98 us  [layer(): pieces = lax.all_to_all(product, out_group, 0, 0, tiled=True)]
    all_to_all x1 -> x2, waiting for transfers between devices: 13.8 us -> 10.9 us  [layer(): pieces = lax.all_to_all(product, out_group, 0, 0, tiled=True)]
  transfers between devices with their start and end apart: 8 -> 9, of which waited for: 6 -> 7; matrix products, arithmetic and copies ran while one was open for 4% -> 21% of each run, Pallas kernels for 21% -> 21%
where the time goes in v2:
time: 173 us; the launch traced here: 172 us
  Pallas kernels  45.3 us (26%)
  waiting for transfers between devices  44.4 us (26%)
  local copies, waits for them, and re-layouts  32.2 us (19%)
  starting transfers between devices  23.3 us (13%)
  matrix products  14.7 us (8%)
  other arithmetic  7.81 us (5%)
  between operations  4.17 us (2%)
    unnamed x17, local copies, waits for them, and re-layouts  27.4 us
    pallas_call x1, Pallas kernels, own_attend(): pl.pallas_call(functools.partial(own_kernel, kv_heads, block), out_shape=...  24.6 us
    pallas_call x3, Pallas kernels, shared_attend(): pl.pallas_call(functools.partial(shared_kernel, kv_heads, n_blocks, tree...  20.7 us
    ppermute x4, waiting for transfers between devices, exchange_to_owner(): received.append(lax.ppermute(piece, ('req', 'seq'), pairs))  20.5 us
    dot_general x2, matrix products, layer(): jnp.einsum('ik,kcj->cij', attended, blocked[:, :, lo:lo + half], preferre...  13.7 us
    ppermute x2, waiting for transfers between devices, exchange_shared(): received.append(lax.ppermute(sent, 'req', pairs))  12.9 us
    all_to_all x2, waiting for transfers between devices, layer(): pieces = lax.all_to_all(product, out_group, 0, 0, tiled=True)  10.9 us
    ppermute x4, starting transfers between devices, exchange_to_owner(): received.append(lax.ppermute(piece, ('req', 'seq'), pairs))  9.64 us
  transfers between devices with their start and end apart: 9, of which 7 were waited for; matrix products, arithmetic and copies ran while one was open for 21% of the time, Pallas kernels for 21%

profile of v2, /device:TPU:8, one launch (start us, length us, event | category | flops | bytes accessed | tf_op | source)
XLA Modules:
  0.0 171.8 jit_solution(7644340006261633694)
XLA Ops:
  0.6 0.0 copy-start.5
  0.6 1.4 fusion.35
  4.6 3.4 %bitcast_select_fusion = (bf16[2,1,512,512]{3,2,0,1:T(8,128)(2,1)S(1)}, bf16[2,512,512]{2,1,0:T(8,128)(2,1)}, bf16[2,512,512]{2,1,0:T(8,128)(2,1)}, bf16[2,512,512]{2,1,0:T(8,128)(2,1)}) fusion(pred[]{:T(512)S(6)} %eq.74, bf16[2,2,512,512]{3,2,1,0:T(8,128)(2,1)} %param.12, pred[]{:T(512)S(6)} %eq.71, pred[]{:T(512)S(6)} %eq.63, pred[]{:T(512)S(6)} %eq.60), kind=kLoop, calls=%fused_computation.17 | loop fusion | flops 2097152 | bytes 6291460 | tf_op jit(solution)/shard_map/jit(_where)/select_n | solution.py:204
  8.0 0.0 collective-permute-start
  8.0 3.0 %collective-permute-start.1 = (bf16[2,512,512]{2,1,0:T(8,128)(2,1)}, bf16[2,512,512]{2,1,0:T(8,128)(2,1)S(1)}, u32[]{:S(2)}, u32[]{:S(2)}) collective-permute-start(bf16[2,512,512]{2,1,0:T(8,128)(2,1)} %get-tuple-element.33), channel_id=1, source_target_pairs={{0,8},{4,12},{8,0},{12,4},{1,9},{5,13},{9,1},{13,5},{2,10},{6,14},... | collective-permute-start | bytes 3145736 | tf_op jit(solution)/shard_map/ppermute | solution.py:219
  11.7 1.1 copy.37
  12.9 1.0 copy.17
  13.9 0.2 convolution_minimum_fusion.5
  14.1 0.2 convolution_minimum_fusion.4
  14.3 0.2 convolution_minimum_fusion.3
  14.5 0.2 convolution_minimum_fusion.2
  14.6 0.2 convolution_minimum_fusion.1
  14.8 0.2 fusion.17
  15.0 0.9 broadcast_in_dim.37.ones_ref
  15.9 24.6 %shard_map.104 = (f32[4,512,1]{2,1,0:T(8,128)}, f32[4,512,128]{2,1,0:T(8,128)}, f32[4,512,128]{2,1,0:T(8,128)}) custom-call(s32[1]{0:T(128)} %bitcast.5.nv_ref, bf16[4,512,128]{2,1,0:T(8,128)(2,1)} %bitcast.94, bf16[2,8192,512]{2,1,0:T(8,128)(2,1)} %bitcast.112, bf16[2048,128]{1,0:T(8,128)(2,1)} %broadcast_in_dim.37.ones_ref), custom_call_target="tpu_custom_call" | custom-call | flops 12884901888 | bytes 17301504 | tf_op jit(solution)/shard_map/pallas_call | solution.py:96
  40.5 12.9 %collective-permute-done.rest_1_ = bf16[2,512,512]{2,1,0:T(8,128)(2,1)} collective-permute-done((bf16[2,512,512]{2,1,0:T(8,128)(2,1)}, bf16[2,512,512]{2,1,0:T(8,128)(2,1)}, u32[]{:S(2)}, u32[]{:S(2)}) %collective-permute-start) | collective-permute-done | bytes 1048608 | tf_op jit(solution)/shard_map/ppermute | solution.py:219
  53.5 1.2 copy-done.1
  54.7 11.3 %shard_map.105 = (f32[4,512,1]{2,1,0:T(8,128)S(1)}, f32[4,512,128]{2,1,0:T(8,128)S(1)}, f32[4,512,128]{2,1,0:T(8,128)S(1)}) custom-call(s32[1]{0:T(128)} %bitcast.3.flag_ref, bf16[4,512,128]{2,1,0:T(8,128)(2,1)S(1)} %bitcast.95, f32[4,512,1]{2,1,0:T(8,128)S(1)} %copy-done.1, f32[4,512,128]{2,1,0:T(8,128)} %get-tuple-element.14.l_ref, ...), custom_call_target="tpu_custom_call" | custom-call | flops 1610612736 | bytes 2621440 | tf_op jit(solution)/shard_map/pallas_call | solution.py:170
  66.1 1.0 copy-done.2
  67.1 0.0 collective-permute-done.1.rest_0_
  67.1 1.0 copy-done.4
  68.1 5.7 %shard_map.106 = (f32[4,512,1]{2,1,0:T(8,128)S(1)}, f32[4,512,128]{2,1,0:T(8,128)S(1)}, f32[4,512,128]{2,1,0:T(8,128)S(1)}) custom-call(s32[1]{0:T(128)} %constant.18.clone.1.flag_ref, bf16[4,512,128]{2,1,0:T(8,128)(2,1)S(1)} %bitcast.96, f32[4,512,1]{2,1,0:T(8,128)S(1)} %get-tuple-element.16.m_ref, f32[4,512,128]{2,1,0:T(8,128)S(1)} %get-tuple-element.17.l_ref, ...), custom_call_target="tpu_custom_call" | custom-call | flops 805306368 | bytes 1572864 | tf_op jit(solution)/shard_map/pallas_call | solution.py:170
  73.8 0.3 slice_reduce_fusion
  74.2 0.1 divide_convert_fusion
  74.3 0.3 reduce.3
  74.7 0.1 reshape_squeeze.10
  74.8 0.1 maximum_bitcast_fusion.1
  74.9 0.1 reshape_squeeze.11
  75.0 0.1 maximum_bitcast_fusion.2
  75.1 0.9 pad_maximum_fusion
  75.9 3.7 %all-to-all-start = ((bf16[32,66,128]{2,1,0:T(8,128)(2,1)}), bf16[32,66,128]{2,1,0:T(8,128)(2,1)S(1)}, u32[]{:S(2)}, u32[]{:S(2)}) async-start(bf16[32,66,128]{2,1,0:T(8,128)(2,1)} %pad_maximum_fusion), calls=%async_computation | async-start | bytes 1179648 | tf_op jit(solution)/shard_map/all_to_all | solution.py:303
  79.6 0.9 dynamic-slice_bitcast_fusion
  80.5 6.7 %collective-permute-start.2 = (bf16[2,512,128]{2,1,0:T(8,128)(2,1)}, bf16[2,512,128]{2,1,0:T(8,128)(2,1)S(1)}, u32[]{:S(2)}, u32[]{:S(2)}) collective-permute-start(bf16[2,512,128]{2,1,0:T(8,128)(2,1)} %get-tuple-element.39), channel_id=1, source_target_pairs={{0,12},{1,13},{2,14},{3,15},{4,8},{5,9},{6,10},{7,11},{8,4},{9,5},... | collective-permute-start | bytes 786440 | tf_op jit(solution)/shard_map/ppermute | solution.py:234
  87.2 0.0 collective-permute-start.3
  87.2 2.7 %collective-permute-start.4 = (bf16[2,512,128]{2,1,0:T(8,128)(2,1)S(1)}, bf16[2,512,128]{2,1,0:T(8,128)(2,1)S(1)}, u32[]{:S(2)}, u32[]{:S(2)}) collective-permute-start(bf16[2,512,128]{2,1,0:T(8,128)(2,1)S(1)} %get-tuple-element.37), channel_id=1, source_target_pairs={{0,14},{1,15},{2,12},{3,13},{4,10},{5,11},{6,8},{7,9},{8,6},{9,7},... | collective-permute-start | bytes 786440 | tf_op jit(solution)/shard_map/ppermute | solution.py:234
  89.9 0.3 collective-permute-start.5
  90.2 22.4 %copy.26 = bf16[1024,8192]{0,1:T(8,128)(2,1)} copy(bf16[1024,8192]{1,0:T(8,128)(2,1)} %param.13) | data formatting | bytes 33554432 | tf_op args[4]
  112.6 0.0 all-to-all-done
  112.6 0.1 fusion.39
  112.7 0.1 fusion.26
  112.9 0.2 reshape.151.m_ref
  113.1 0.1 broadcast_in_dim.40
  113.1 0.3 multiply_reduce_fusion
  113.5 3.0 %collective-permute-done.2.rest_0_ = bf16[2,512,128]{2,1,0:T(8,128)(2,1)S(1)} collective-permute-done((bf16[2,512,128]{2,1,0:T(8,128)(2,1)}, bf16[2,512,128]{2,1,0:T(8,128)(2,1)S(1)}, u32[]{:S(2)}, u32[]{:S(2)}) %collective-permute-start.2) | collective-permute-done | bytes 262176 | tf_op jit(solution)/shard_map/ppermute | solution.py:234
  116.5 5.5 %collective-permute-done.3.rest_1_ = bf16[2,512,128]{2,1,0:T(8,128)(2,1)S(1)} collective-permute-done((bf16[2,512,128]{2,1,0:T(8,128)(2,1)S(1)}, bf16[2,512,128]{2,1,0:T(8,128)(2,1)S(1)}, u32[]{:S(2)}, u32[]{:S(2)}) %collective-permute-start.3) | collective-permute-done | bytes 262176 | tf_op jit(solution)/shard_map/ppermute | solution.py:234
  122.0 6.5 %collective-permute-done.4.rest_2_ = bf16[2,512,128]{2,1,0:T(8,128)(2,1)S(1)} collective-permute-done((bf16[2,512,128]{2,1,0:T(8,128)(2,1)S(1)}, bf16[2,512,128]{2,1,0:T(8,128)(2,1)S(1)}, u32[]{:S(2)}, u32[]{:S(2)}) %collective-permute-start.4) | collective-permute-done | bytes 262176 | tf_op jit(solution)/shard_map/ppermute | solution.py:234
  128.5 5.5 %collective-permute-done.5.rest_3_ = bf16[2,512,128]{2,1,0:T(8,128)(2,1)S(1)} collective-permute-done((bf16[2,512,128]{2,1,0:T(8,128)(2,1)S(1)}, bf16[2,512,128]{2,1,0:T(8,128)(2,1)S(1)}, u32[]{:S(2)}, u32[]{:S(2)}) %collective-permute-start.5) | collective-permute-done | bytes 262176 | tf_op jit(solution)/shard_map/ppermute | solution.py:234
  134.0 0.1 broadcast_in_dim.41.l_ref
  134.1 3.6 %shard_map.107 = (f32[1,512,1]{2,1,0:T(8,128)}, f32[1,512,128]{2,1,0:T(8,128)S(1)}, f32[1,512,128]{2,1,0:T(8,128)S(1)}) custom-call(s32[1]{0:T(128)} %constant.18.clone.1.flag_ref, bf16[1,512,128]{2,1,0:T(8,128)(2,1)S(1)} %constant_dynamic-slice_fusion.q_ref, f32[1,512,1]{2,1,0:T(8,128)S(1)} %reshape.151.m_ref, f32[1,512,128]{2,1,0:T(8,128)S(1)} %broadcast_in_dim.41.l_ref, ...), custom_call_target="tpu_custom_call" | custom-call | flops 805306368 | bytes 1179648 | tf_op jit(solution)/shard_map/pallas_call | solution.py:170
  137.8 0.1 copy.25
  137.9 0.1 reshape.150
  137.9 6.9 %fusion.13 = bf16[8,64,512]{2,1,0:T(8,128)(2,1)} fusion(bf16[64,1024,1]{1,0,2:T(8,128)(2,1)S(1)} %reshape.150, bf16[1024,8,1024]{0,2,1:T(8,128)(2,1)} %bitcast.102), kind=kOutput, calls=%fused_computation.8 | convolution fusion | flops 537133056 | bytes 9043968 | tf_op jit(solution)/shard_map/ik,kcj->cij/dot_general | solution.py:334
  144.8 3.5 %all-to-all-start.1 = ((bf16[8,64,512]{2,1,0:T(8,128)(2,1)}), bf16[8,64,512]{2,1,0:T(8,128)(2,1)S(1)}, u32[]{:S(2)}, u32[]{:S(2)}) async-start(bf16[8,64,512]{2,1,0:T(8,128)(2,1)} %fusion.13), calls=%async_computation.1 | async-start | bytes 1048576 | tf_op jit(solution)/shard_map/all_to_all | solution.py:340
  148.3 6.8 %fusion.10 = bf16[8,64,512]{2,1,0:T(8,128)(2,1)} fusion(bf16[64,1024,1]{1,0,2:T(8,128)(2,1)S(1)} %reshape.150, bf16[1024,8,1024]{0,2,1:T(8,128)(2,1)} %bitcast.103), kind=kOutput, calls=%fused_computation.7 | convolution fusion | flops 537133056 | bytes 9043968 | tf_op jit(solution)/shard_map/ik,kcj->cij/dot_general | solution.py:334
  155.1 2.8 %all-to-all-done.1 = bf16[8,64,512]{2,1,0:T(8,128)(2,1)S(1)} async-done(((bf16[8,64,512]{2,1,0:T(8,128)(2,1)}), bf16[8,64,512]{2,1,0:T(8,128)(2,1)S(1)}, u32[]{:S(2)}, u32[]{:S(2)}) %all-to-all-start.1) | async-done | bytes 524320 | tf_op jit(solution)/shard_map/all_to_all | solution.py:340
  157.9 3.5 %all-to-all-start.2 = ((bf16[8,64,512]{2,1,0:T(8,128)(2,1)}), bf16[8,64,512]{2,1,0:T(8,128)(2,1)S(1)}, u32[]{:S(2)}, u32[]{:S(2)}) async-start(bf16[8,64,512]{2,1,0:T(8,128)(2,1)} %fusion.10), calls=%async_computation.2 | async-start | bytes 1048576 | tf_op jit(solution)/shard_map/all_to_all | solution.py:340
  161.5 0.1 copy.29
  161.6 0.6 gather_fusion
  162.2 0.1 broadcast_select_fusion
  162.3 0.6 copy.30
  162.9 0.1 reduce_sum.84
  163.0 8.1 %all-to-all-done.2 = bf16[8,64,512]{2,1,0:T(8,128)(2,1)S(1)} async-done(((bf16[8,64,512]{2,1,0:T(8,128)(2,1)}), bf16[8,64,512]{2,1,0:T(8,128)(2,1)S(1)}, u32[]{:S(2)}, u32[]{:S(2)}) %all-to-all-start.2) | async-done | bytes 524320 | tf_op jit(solution)/shard_map/all_to_all | solution.py:340
  171.1 0.1 reduce_sum.85
  171.2 0.7 maximum_bitcast_fusion
  (24 shorter events, 0.2 us)
Async XLA Ops:
  0.6 13.2 %copy-start.5 = (s32[1,64]{1,0:T(1,128)S(1)}, s32[1,64]{1,0:T(1,128)}, u32[]{:S(2)}) copy-start(s32[1,64]{1,0:T(1,128)} %param.16) | copy-start | bytes 772
  8.0 45.4 %collective-permute-start = (bf16[2,512,512]{2,1,0:T(8,128)(2,1)}, bf16[2,512,512]{2,1,0:T(8,128)(2,1)}, u32[]{:S(2)}, u32[]{:S(2)}) collective-permute-start(bf16[2,512,512]{2,1,0:T(8,128)(2,1)} %get-tuple-element.34), channel_id=1, source_target_pairs={{0,4},{4,0},{8,12},{12,8},{1,5},{5,1},{9,13},{13,9},{2,6},{6,2},{1... | collective-permute-start | bytes 3145736 | tf_op jit(solution)/shard_map/ppermute | solution.py:219
  8.0 59.0 %collective-permute-start.1 = (bf16[2,512,512]{2,1,0:T(8,128)(2,1)}, bf16[2,512,512]{2,1,0:T(8,128)(2,1)S(1)}, u32[]{:S(2)}, u32[]{:S(2)}) collective-permute-start(bf16[2,512,512]{2,1,0:T(8,128)(2,1)} %get-tuple-element.33), channel_id=1, source_target_pairs={{0,8},{4,12},{8,0},{12,4},{1,9},{5,13},{9,1},{13,5},{2,10},{6,14},... | collective-permute-start | bytes 3145736 | tf_op jit(solution)/shard_map/ppermute | solution.py:219
  15.9 37.6 %copy-start = (bf16[64,4,8,128]{3,0,2,1:T(8,128)(2,1)S(1)}, bf16[64,4,8,128]{3,0,2,1:T(8,128)(2,1)}, u32[]{:S(2)}) copy-start(bf16[64,4,8,128]{3,0,2,1:T(8,128)(2,1)} %copy.17) | copy-start | bytes 1572868
  15.9 37.6 %copy-start.3 = (bf16[1,2,64,512]{3,2,1,0:T(8,128)(2,1)S(1)}, bf16[1,2,64,512]{3,2,1,0:T(8,128)(2,1)}, u32[]{:S(2)}) copy-start(bf16[1,2,64,512]{3,2,1,0:T(8,128)(2,1)} %param.10) | copy-start | bytes 393220
  53.5 1.2 copy-start.1
  66.0 1.0 copy-start.2
  67.1 1.0 copy-start.4
  75.9 36.7 %all-to-all-start = ((bf16[32,66,128]{2,1,0:T(8,128)(2,1)}), bf16[32,66,128]{2,1,0:T(8,128)(2,1)S(1)}, u32[]{:S(2)}, u32[]{:S(2)}) async-start(bf16[32,66,128]{2,1,0:T(8,128)(2,1)} %pad_maximum_fusion), calls=%async_computation | async-start | bytes 1179648 | tf_op jit(solution)/shard_map/all_to_all | solution.py:303
  80.5 36.0 %collective-permute-start.2 = (bf16[2,512,128]{2,1,0:T(8,128)(2,1)}, bf16[2,512,128]{2,1,0:T(8,128)(2,1)S(1)}, u32[]{:S(2)}, u32[]{:S(2)}) collective-permute-start(bf16[2,512,128]{2,1,0:T(8,128)(2,1)} %get-tuple-element.39), channel_id=1, source_target_pairs={{0,12},{1,13},{2,14},{3,15},{4,8},{5,9},{6,10},{7,11},{8,4},{9,5},... | collective-permute-start | bytes 786440 | tf_op jit(solution)/shard_map/ppermute | solution.py:234
  87.2 34.8 %collective-permute-start.3 = (bf16[2,512,128]{2,1,0:T(8,128)(2,1)S(1)}, bf16[2,512,128]{2,1,0:T(8,128)(2,1)S(1)}, u32[]{:S(2)}, u32[]{:S(2)}) collective-permute-start(bf16[2,512,128]{2,1,0:T(8,128)(2,1)S(1)} %get-tuple-element.38), channel_id=1, source_target_pairs={{0,13},{1,12},{2,15},{3,14},{4,9},{5,8},{6,11},{7,10},{8,5},{9,4},... | collective-permute-start | bytes 786440 | tf_op jit(solution)/shard_map/ppermute | solution.py:234
  87.2 41.3 %collective-permute-start.4 = (bf16[2,512,128]{2,1,0:T(8,128)(2,1)S(1)}, bf16[2,512,128]{2,1,0:T(8,128)(2,1)S(1)}, u32[]{:S(2)}, u32[]{:S(2)}) collective-permute-start(bf16[2,512,128]{2,1,0:T(8,128)(2,1)S(1)} %get-tuple-element.37), channel_id=1, source_target_pairs={{0,14},{1,15},{2,12},{3,13},{4,10},{5,11},{6,8},{7,9},{8,6},{9,7},... | collective-permute-start | bytes 786440 | tf_op jit(solution)/shard_map/ppermute | solution.py:234
  89.9 44.1 %collective-permute-start.5 = (bf16[2,512,128]{2,1,0:T(8,128)(2,1)S(1)}, bf16[2,512,128]{2,1,0:T(8,128)(2,1)S(1)}, u32[]{:S(2)}, u32[]{:S(2)}) collective-permute-start(bf16[2,512,128]{2,1,0:T(8,128)(2,1)S(1)} %get-tuple-element.36), channel_id=1, source_target_pairs={{0,15},{1,14},{2,13},{3,12},{4,11},{5,10},{6,9},{7,8},{8,7},{9,6},... | collective-permute-start | bytes 786440 | tf_op jit(solution)/shard_map/ppermute | solution.py:234
  90.2 22.5 %copy-start.6 = (s32[1,8]{1,0:T(1,128)S(1)}, s32[1,8]{1,0:T(1,128)}, u32[]{:S(2)}) copy-start(s32[1,8]{1,0:T(1,128)} %param.17) | copy-start | bytes 100
  144.8 13.1 %all-to-all-start.1 = ((bf16[8,64,512]{2,1,0:T(8,128)(2,1)}), bf16[8,64,512]{2,1,0:T(8,128)(2,1)S(1)}, u32[]{:S(2)}, u32[]{:S(2)}) async-start(bf16[8,64,512]{2,1,0:T(8,128)(2,1)} %fusion.13), calls=%async_computation.1 | async-start | bytes 1048576 | tf_op jit(solution)/shard_map/all_to_all | solution.py:340
  157.9 13.1 %all-to-all-start.2 = ((bf16[8,64,512]{2,1,0:T(8,128)(2,1)}), bf16[8,64,512]{2,1,0:T(8,128)(2,1)S(1)}, u32[]{:S(2)}, u32[]{:S(2)}) async-start(bf16[8,64,512]{2,1,0:T(8,128)(2,1)} %fusion.10), calls=%async_computation.2 | async-start | bytes 1048576 | tf_op jit(solution)/shard_map/all_to_all | solution.py:340

commit v3 on v0

--- a/solution.py
+++ b/solution.py
@@ -13,7 +13,7 @@
 NEG_FILL = -1e30
 SCALE = HD ** (-0.5)
 EXP2_SCALE = SCALE * 1.4426950408889634
-OWN_BLOCK = 1024
+OWN_BLOCK = 2048
 
 
 def step(m_prev, l_prev, acc_prev, q, k, v, ones, ok):
@@ -50,8 +50,9 @@
         if masked:
             cols = start + lax.broadcasted_iota(jnp.int32, (1, block), 1)
             ok = cols < n_valid
-        for h in range(kv_heads):
-            cols_h = slice(h * HD, (h + 1) * HD)
+
+        def head(h, carry):
+            cols_h = pl.ds(pl.multiple_of(h * HD, HD), HD)
             m, l, acc = step(
                 m_s[h], l_s[h], acc_s[h], q_ref[h], kv_ref[0, :, cols_h], kv_ref[1, :, cols_h],
                 ones_ref[...], ok,
@@ -59,6 +60,9 @@
             m_s[h] = m
             l_s[h] = l
             acc_s[h] = acc
+            return carry
+
+        lax.fori_loop(0, kv_heads, head, 0)
 
     full = start + block <= n_valid
     part = jnp.logical_and(start < n_valid, jnp.logical_not(full))
@@ -120,8 +124,9 @@
         dkv_ref, reach_ref, tree_ones_ref = rest[:3]
         rest = rest[3:]
     m_out, l_out, acc_out = rest[:3]
-    for h in range(kv_heads):
-        cols_h = slice(h * HD, (h + 1) * HD)
+
+    def head(h, carry):
+        cols_h = pl.ds(pl.multiple_of(h * HD, HD), HD)
         q = q_ref[h]
         m, l, acc = m_ref[h], l_ref[h], acc_ref[h]
         for blk in blocks:
@@ -131,6 +136,9 @@
         m_out[h] = m
         l_out[h] = l
         acc_out[h] = acc
+        return carry
+
+    lax.fori_loop(0, kv_heads, head, 0)
 
     if with_tree:
         @pl.when(flag_ref[0] == 1)
@@ -278,8 +286,8 @@
     reach = tree_reach(parents[0])
     reach_rows = jnp.tile(reach.astype(jnp.float32), (QPK, 1))
     flag = (seq_index == 0).astype(jnp.int32).reshape(1)
-    state = shared_attend(queries, state, blocks[:1], (draft_kv[0], reach_rows, flag))
-    for blk in blocks[1:]:
+    state = shared_attend(queries, state, blocks[:2], (draft_kv[0], reach_rows, flag))
+    for blk in blocks[2:]:
         state = shared_attend(queries, state, [blk])
     m, l, acc = state
 

time: 172 us -> 166 us (0.965)
  starting transfers between devices: 34.4 us -> 18.9 us
  waiting for transfers between devices: 64.8 us -> 70.8 us
  Pallas kernels: 41.8 us -> 45.3 us
    ppermute x4, starting transfers between devices: 24 us -> 8.54 us  [exchange_to_owner(): received.append(lax.ppermute(piece, ('req', 'seq'), pairs))]
    ppermute x2, waiting for transfers between devices: 7.99 us -> 14 us  [exchange_shared(): received.append(lax.ppermute(sent, 'req', pairs))]
    pallas_call x1, Pallas kernels: 21.6 us -> 24.6 us  [own_attend(): pl.pallas_call(functools.partial(own_kernel, kv_heads, block), out_shape=...]
    unnamed x20 -> x18, local copies, waits for them, and re-layouts: 4.9 us -> 3.96 us
    pallas_call x4 -> x3, Pallas kernels: 20.2 us -> 20.7 us  [shared_attend(): pl.pallas_call(functools.partial(shared_kernel, kv_heads, n_blocks, tree...]
  transfers between devices with their start and end apart: 8 -> 8, of which waited for: 6 -> 6; matrix products, arithmetic and copies ran while one was open for 4% -> 4% of each run, Pallas kernels for 19% -> 22%
where the time goes in v3:
time: 166 us; the launch traced here: 165 us
  waiting for transfers between devices  70.8 us (43%)
  Pallas kernels  45.3 us (27%)
  starting transfers between devices  18.9 us (11%)
  matrix products  9.48 us (6%)
  local copies, waits for them, and re-layouts  8.67 us (5%)
  other arithmetic  7.9 us (5%)
  between operations  4.17 us (3%)
    ppermute x4, waiting for transfers between devices, exchange_to_owner(): received.append(lax.ppermute(piece, ('req', 'seq'), pairs))  43 us
    pallas_call x1, Pallas kernels, own_attend(): pl.pallas_call(functools.partial(own_kernel, kv_heads, block), out_shape=...  24.6 us
    pallas_call x3, Pallas kernels, shared_attend(): pl.pallas_call(functools.partial(shared_kernel, kv_heads, n_blocks, tree...  20.7 us
    ppermute x2, waiting for transfers between devices, exchange_shared(): received.append(lax.ppermute(sent, 'req', pairs))  14 us
    all_to_all x1, waiting for transfers between devices, layer(): pieces = lax.all_to_all(product, out_group, 0, 0, tiled=True)  13.8 us
    ppermute x4, starting transfers between devices, exchange_to_owner(): received.append(lax.ppermute(piece, ('req', 'seq'), pairs))  8.54 us
    dot_general x1, matrix products, layer(): jnp.einsum('ik,kcj->cij', attended, out_weight.reshape(out_weight.shape[0...  8.44 us
    unnamed x18, local copies, waits for them, and re-layouts  3.96 us
  transfers between devices with their start and end apart: 8, of which 6 were waited for; matrix products, arithmetic and copies ran while one was open for 4% of the time, Pallas kernels for 22%

profile of v3, /device:TPU:8, one launch (start us, length us, event | category | flops | bytes accessed | tf_op | source)
XLA Modules:
  0.0 165.2 jit_solution(10846280614959202475)
XLA Ops:
  0.6 1.4 fusion.28
  4.6 0.0 copy-start.5
  4.6 3.5 %bitcast_select_fusion = (bf16[2,1,512,512]{3,2,0,1:T(8,128)(2,1)S(1)}, bf16[2,512,512]{2,1,0:T(8,128)(2,1)}, bf16[2,512,512]{2,1,0:T(8,128)(2,1)}, bf16[2,512,512]{2,1,0:T(8,128)(2,1)}) fusion(pred[]{:T(512)S(6)} %eq.74, bf16[2,2,512,512]{3,2,1,0:T(8,128)(2,1)} %param.12, pred[]{:T(512)S(6)} %eq.71, pred[]{:T(512)S(6)} %eq.63, pred[]{:T(512)S(6)} %eq.60), kind=kLoop, calls=%fused_computation.14 | loop fusion | flops 2097152 | bytes 6291460 | tf_op jit(solution)/shard_map/jit(_where)/select_n | solution.py:204
  8.1 0.0 collective-permute-start
  8.1 3.0 %collective-permute-start.1 = (bf16[2,512,512]{2,1,0:T(8,128)(2,1)}, bf16[2,512,512]{2,1,0:T(8,128)(2,1)S(1)}, u32[]{:S(2)}, u32[]{:S(2)}) collective-permute-start(bf16[2,512,512]{2,1,0:T(8,128)(2,1)} %get-tuple-element.33), channel_id=1, source_target_pairs={{0,8},{4,12},{8,0},{12,4},{1,9},{5,13},{9,1},{13,5},{2,10},{6,14},... | collective-permute-start | bytes 3145736 | tf_op jit(solution)/shard_map/ppermute | solution.py:219
  11.8 0.0 copy-done.5
  11.8 0.1 copy.35
  11.9 1.0 copy.18
  12.9 0.0 copy-done.6
  12.9 0.2 convolution_minimum_fusion.5
  13.1 0.2 convolution_minimum_fusion.4
  13.3 0.2 convolution_minimum_fusion.3
  13.5 0.2 convolution_minimum_fusion.2
  13.7 0.2 convolution_minimum_fusion.1
  13.8 0.2 fusion.10
  14.0 0.9 broadcast_in_dim.37.ones_ref
  14.9 24.6 %shard_map.104 = (f32[4,512,1]{2,1,0:T(8,128)}, f32[4,512,128]{2,1,0:T(8,128)}, f32[4,512,128]{2,1,0:T(8,128)}) custom-call(s32[1]{0:T(128)} %bitcast.5.nv_ref, bf16[4,512,128]{2,1,0:T(8,128)(2,1)} %bitcast.97, bf16[2,8192,512]{2,1,0:T(8,128)(2,1)} %bitcast.114, bf16[2048,128]{1,0:T(8,128)(2,1)} %broadcast_in_dim.37.ones_ref), custom_call_target="tpu_custom_call" | custom-call | flops 12884901888 | bytes 17301504 | tf_op jit(solution)/shard_map/pallas_call | solution.py:96
  39.5 14.0 %collective-permute-done.rest_1_ = bf16[2,512,512]{2,1,0:T(8,128)(2,1)} collective-permute-done((bf16[2,512,512]{2,1,0:T(8,128)(2,1)}, bf16[2,512,512]{2,1,0:T(8,128)(2,1)}, u32[]{:S(2)}, u32[]{:S(2)}) %collective-permute-start) | collective-permute-done | bytes 1048608 | tf_op jit(solution)/shard_map/ppermute | solution.py:219
  53.5 0.0 copy-done
  53.5 0.0 copy-done.3
  53.6 0.0 copy-start.1
  53.6 1.2 copy-done.1
  54.8 11.3 %shard_map.105 = (f32[4,512,1]{2,1,0:T(8,128)S(1)}, f32[4,512,128]{2,1,0:T(8,128)S(1)}, f32[4,512,128]{2,1,0:T(8,128)S(1)}) custom-call(s32[1]{0:T(128)} %bitcast.3.flag_ref, bf16[4,512,128]{2,1,0:T(8,128)(2,1)S(1)} %bitcast.98, f32[4,512,1]{2,1,0:T(8,128)S(1)} %copy-done.1, f32[4,512,128]{2,1,0:T(8,128)} %get-tuple-element.14.l_ref, ...), custom_call_target="tpu_custom_call" | custom-call | flops 1610612736 | bytes 2621440 | tf_op jit(solution)/shard_map/pallas_call | solution.py:170
  66.1 0.0 copy-start.2
  66.1 1.0 copy-done.2
  67.1 0.0 collective-permute-done.1.rest_0_
  67.1 1.0 copy-done.4
  68.1 5.7 %shard_map.106 = (f32[4,512,1]{2,1,0:T(8,128)S(1)}, f32[4,512,128]{2,1,0:T(8,128)S(1)}, f32[4,512,128]{2,1,0:T(8,128)S(1)}) custom-call(s32[1]{0:T(128)} %constant.17.clone.1.flag_ref, bf16[4,512,128]{2,1,0:T(8,128)(2,1)S(1)} %bitcast.99, f32[4,512,1]{2,1,0:T(8,128)S(1)} %get-tuple-element.16.m_ref, f32[4,512,128]{2,1,0:T(8,128)S(1)} %get-tuple-element.17.l_ref, ...), custom_call_target="tpu_custom_call" | custom-call | flops 805306368 | bytes 1572864 | tf_op jit(solution)/shard_map/pallas_call | solution.py:170
  73.9 0.3 slice_reduce_fusion
  74.2 0.1 divide_convert_fusion
  74.4 0.3 reduce.2
  74.7 0.1 reshape_squeeze.10
  74.8 0.1 maximum_bitcast_fusion
  74.9 0.1 reshape_squeeze.11
  75.0 0.1 maximum_bitcast_fusion.1
  75.1 0.9 pad_maximum_fusion
  76.0 3.7 %all-to-all-start = ((bf16[32,66,128]{2,1,0:T(8,128)(2,1)}), bf16[32,66,128]{2,1,0:T(8,128)(2,1)S(1)}, u32[]{:S(2)}, u32[]{:S(2)}) async-start(bf16[32,66,128]{2,1,0:T(8,128)(2,1)} %pad_maximum_fusion), calls=%async_computation | async-start | bytes 1179648 | tf_op jit(solution)/shard_map/all_to_all | solution.py:303
  79.7 0.9 dynamic-slice_bitcast_fusion
  80.6 5.6 %collective-permute-start.2 = (bf16[2,512,128]{2,1,0:T(8,128)(2,1)}, bf16[2,512,128]{2,1,0:T(8,128)(2,1)S(1)}, u32[]{:S(2)}, u32[]{:S(2)}) collective-permute-start(bf16[2,512,128]{2,1,0:T(8,128)(2,1)} %get-tuple-element.39), channel_id=1, source_target_pairs={{0,12},{1,13},{2,14},{3,15},{4,8},{5,9},{6,10},{7,11},{8,4},{9,5},... | collective-permute-start | bytes 786440 | tf_op jit(solution)/shard_map/ppermute | solution.py:234
  86.2 0.0 collective-permute-start.3
  86.2 2.7 %collective-permute-start.4 = (bf16[2,512,128]{2,1,0:T(8,128)(2,1)S(1)}, bf16[2,512,128]{2,1,0:T(8,128)(2,1)S(1)}, u32[]{:S(2)}, u32[]{:S(2)}) collective-permute-start(bf16[2,512,128]{2,1,0:T(8,128)(2,1)S(1)} %get-tuple-element.37), channel_id=1, source_target_pairs={{0,14},{1,15},{2,12},{3,13},{4,10},{5,11},{6,8},{7,9},{8,6},{9,7},... | collective-permute-start | bytes 786440 | tf_op jit(solution)/shard_map/ppermute | solution.py:234
  88.8 0.3 collective-permute-start.5
  89.1 0.0 all-to-all-done
  89.1 0.1 fusion.32
  89.2 0.1 fusion.19
  89.4 0.2 reshape.151.m_ref
  89.6 0.1 broadcast_in_dim.40
  89.7 0.3 multiply_reduce_fusion
  90.0 25.5 %collective-permute-done.2.rest_0_ = bf16[2,512,128]{2,1,0:T(8,128)(2,1)S(1)} collective-permute-done((bf16[2,512,128]{2,1,0:T(8,128)(2,1)}, bf16[2,512,128]{2,1,0:T(8,128)(2,1)S(1)}, u32[]{:S(2)}, u32[]{:S(2)}) %collective-permute-start.2) | collective-permute-done | bytes 262176 | tf_op jit(solution)/shard_map/ppermute | solution.py:234
  115.5 5.5 %collective-permute-done.3.rest_1_ = bf16[2,512,128]{2,1,0:T(8,128)(2,1)S(1)} collective-permute-done((bf16[2,512,128]{2,1,0:T(8,128)(2,1)S(1)}, bf16[2,512,128]{2,1,0:T(8,128)(2,1)S(1)}, u32[]{:S(2)}, u32[]{:S(2)}) %collective-permute-start.3) | collective-permute-done | bytes 262176 | tf_op jit(solution)/shard_map/ppermute | solution.py:234
  121.0 6.5 %collective-permute-done.4.rest_2_ = bf16[2,512,128]{2,1,0:T(8,128)(2,1)S(1)} collective-permute-done((bf16[2,512,128]{2,1,0:T(8,128)(2,1)S(1)}, bf16[2,512,128]{2,1,0:T(8,128)(2,1)S(1)}, u32[]{:S(2)}, u32[]{:S(2)}) %collective-permute-start.4) | collective-permute-done | bytes 262176 | tf_op jit(solution)/shard_map/ppermute | solution.py:234
  127.5 5.5 %collective-permute-done.5.rest_3_ = bf16[2,512,128]{2,1,0:T(8,128)(2,1)S(1)} collective-permute-done((bf16[2,512,128]{2,1,0:T(8,128)(2,1)S(1)}, bf16[2,512,128]{2,1,0:T(8,128)(2,1)S(1)}, u32[]{:S(2)}, u32[]{:S(2)}) %collective-permute-start.5) | collective-permute-done | bytes 262176 | tf_op jit(solution)/shard_map/ppermute | solution.py:234
  133.0 0.1 broadcast_in_dim.41.l_ref
  133.1 3.6 %shard_map.107 = (f32[1,512,1]{2,1,0:T(8,128)}, f32[1,512,128]{2,1,0:T(8,128)S(1)}, f32[1,512,128]{2,1,0:T(8,128)S(1)}) custom-call(s32[1]{0:T(128)} %constant.17.clone.1.flag_ref, bf16[1,512,128]{2,1,0:T(8,128)(2,1)S(1)} %constant_dynamic-slice_fusion.q_ref, f32[1,512,1]{2,1,0:T(8,128)S(1)} %reshape.151.m_ref, f32[1,512,128]{2,1,0:T(8,128)S(1)} %broadcast_in_dim.41.l_ref, ...), custom_call_target="tpu_custom_call" | custom-call | flops 805306368 | bytes 1179648 | tf_op jit(solution)/shard_map/pallas_call | solution.py:170
  136.8 0.1 copy.26
  136.9 0.1 reshape.150
  136.9 8.4 %fusion.6 = bf16[8,64,1024]{2,1,0:T(8,128)(2,1)} fusion(bf16[64,1024,1]{1,0,2:T(8,128)(2,1)S(1)} %reshape.150, bf16[128,8,8,1024]{3,2,1,0:T(8,128)(2,1)} %bitcast.115), kind=kOutput, calls=%fused_computation.5 | convolution fusion | flops 1074266112 | bytes 17956864 | tf_op jit(solution)/shard_map/ik,kcj->cij/dot_general | solution.py:330
  145.4 3.7 %all-to-all-start.1 = ((bf16[8,64,1024]{2,1,0:T(8,128)(2,1)}), bf16[8,64,1024]{2,1,0:T(8,128)(2,1)S(1)}, u32[]{:S(2)}, u32[]{:S(2)}) async-start(bf16[8,64,1024]{2,1,0:T(8,128)(2,1)} %fusion.6), calls=%async_computation.1 | async-start | bytes 2097152 | tf_op jit(solution)/shard_map/all_to_all | solution.py:336
  149.1 0.1 copy.28
  149.2 0.6 gather_fusion
  149.8 0.1 broadcast_select_fusion
  149.9 0.6 copy.29
  150.6 13.8 %all-to-all-done.1 = bf16[8,64,1024]{2,1,0:T(8,128)(2,1)S(1)} async-done(((bf16[8,64,1024]{2,1,0:T(8,128)(2,1)}), bf16[8,64,1024]{2,1,0:T(8,128)(2,1)S(1)}, u32[]{:S(2)}, u32[]{:S(2)}) %all-to-all-start.1) | async-done | bytes 1048608 | tf_op jit(solution)/shard_map/all_to_all | solution.py:336
  164.4 0.8 reduce_sum.72
  (20 shorter events, 0.2 us)
Async XLA Ops:
  4.6 7.2 %copy-start.5 = (bf16[1,64,4096]{2,1,0:T(8,128)(2,1)S(1)}, bf16[1,64,4096]{2,1,0:T(8,128)(2,1)}, u32[]{:S(2)}) copy-start(bf16[1,64,4096]{2,1,0:T(8,128)(2,1)} %param.9) | copy-start | bytes 1572868
  8.1 4.8 %copy-start.6 = (s32[1,64]{1,0:T(1,128)S(1)}, s32[1,64]{1,0:T(1,128)}, u32[]{:S(2)}) copy-start(s32[1,64]{1,0:T(1,128)} %param.16) | copy-start | bytes 772
  8.1 45.4 %collective-permute-start = (bf16[2,512,512]{2,1,0:T(8,128)(2,1)}, bf16[2,512,512]{2,1,0:T(8,128)(2,1)}, u32[]{:S(2)}, u32[]{:S(2)}) collective-permute-start(bf16[2,512,512]{2,1,0:T(8,128)(2,1)} %get-tuple-element.34), channel_id=1, source_target_pairs={{0,4},{4,0},{8,12},{12,8},{1,5},{5,1},{9,13},{13,9},{2,6},{6,2},{1... | collective-permute-start | bytes 3145736 | tf_op jit(solution)/shard_map/ppermute | solution.py:219
  8.1 59.0 %collective-permute-start.1 = (bf16[2,512,512]{2,1,0:T(8,128)(2,1)}, bf16[2,512,512]{2,1,0:T(8,128)(2,1)S(1)}, u32[]{:S(2)}, u32[]{:S(2)}) collective-permute-start(bf16[2,512,512]{2,1,0:T(8,128)(2,1)} %get-tuple-element.33), channel_id=1, source_target_pairs={{0,8},{4,12},{8,0},{12,4},{1,9},{5,13},{9,1},{13,5},{2,10},{6,14},... | collective-permute-start | bytes 3145736 | tf_op jit(solution)/shard_map/ppermute | solution.py:219
  14.9 38.7 %copy-start = (bf16[64,4,8,128]{3,0,2,1:T(8,128)(2,1)S(1)}, bf16[64,4,8,128]{3,0,2,1:T(8,128)(2,1)}, u32[]{:S(2)}) copy-start(bf16[64,4,8,128]{3,0,2,1:T(8,128)(2,1)} %copy.18) | copy-start | bytes 1572868
  14.9 38.7 %copy-start.3 = (bf16[1,2,64,512]{3,2,1,0:T(8,128)(2,1)S(1)}, bf16[1,2,64,512]{3,2,1,0:T(8,128)(2,1)}, u32[]{:S(2)}) copy-start(bf16[1,2,64,512]{3,2,1,0:T(8,128)(2,1)} %param.10) | copy-start | bytes 393220
  53.6 1.2 copy-start.1
  66.1 1.0 copy-start.2
  67.1 1.0 copy-start.4
  76.0 13.1 %all-to-all-start = ((bf16[32,66,128]{2,1,0:T(8,128)(2,1)}), bf16[32,66,128]{2,1,0:T(8,128)(2,1)S(1)}, u32[]{:S(2)}, u32[]{:S(2)}) async-start(bf16[32,66,128]{2,1,0:T(8,128)(2,1)} %pad_maximum_fusion), calls=%async_computation | async-start | bytes 1179648 | tf_op jit(solution)/shard_map/all_to_all | solution.py:303
  80.6 34.9 %collective-permute-start.2 = (bf16[2,512,128]{2,1,0:T(8,128)(2,1)}, bf16[2,512,128]{2,1,0:T(8,128)(2,1)S(1)}, u32[]{:S(2)}, u32[]{:S(2)}) collective-permute-start(bf16[2,512,128]{2,1,0:T(8,128)(2,1)} %get-tuple-element.39), channel_id=1, source_target_pairs={{0,12},{1,13},{2,14},{3,15},{4,8},{5,9},{6,10},{7,11},{8,4},{9,5},... | collective-permute-start | bytes 786440 | tf_op jit(solution)/shard_map/ppermute | solution.py:234
  86.2 34.8 %collective-permute-start.3 = (bf16[2,512,128]{2,1,0:T(8,128)(2,1)S(1)}, bf16[2,512,128]{2,1,0:T(8,128)(2,1)S(1)}, u32[]{:S(2)}, u32[]{:S(2)}) collective-permute-start(bf16[2,512,128]{2,1,0:T(8,128)(2,1)S(1)} %get-tuple-element.38), channel_id=1, source_target_pairs={{0,13},{1,12},{2,15},{3,14},{4,9},{5,8},{6,11},{7,10},{8,5},{9,4},... | collective-permute-start | bytes 786440 | tf_op jit(solution)/shard_map/ppermute | solution.py:234
  86.2 41.3 %collective-permute-start.4 = (bf16[2,512,128]{2,1,0:T(8,128)(2,1)S(1)}, bf16[2,512,128]{2,1,0:T(8,128)(2,1)S(1)}, u32[]{:S(2)}, u32[]{:S(2)}) collective-permute-start(bf16[2,512,128]{2,1,0:T(8,128)(2,1)S(1)} %get-tuple-element.37), channel_id=1, source_target_pairs={{0,14},{1,15},{2,12},{3,13},{4,10},{5,11},{6,8},{7,9},{8,6},{9,7},... | collective-permute-start | bytes 786440 | tf_op jit(solution)/shard_map/ppermute | solution.py:234
  88.8 44.2 %collective-permute-start.5 = (bf16[2,512,128]{2,1,0:T(8,128)(2,1)S(1)}, bf16[2,512,128]{2,1,0:T(8,128)(2,1)S(1)}, u32[]{:S(2)}, u32[]{:S(2)}) collective-permute-start(bf16[2,512,128]{2,1,0:T(8,128)(2,1)S(1)} %get-tuple-element.36), channel_id=1, source_target_pairs={{0,15},{1,14},{2,13},{3,12},{4,11},{5,10},{6,9},{7,8},{8,7},{9,6},... | collective-permute-start | bytes 786440 | tf_op jit(solution)/shard_map/ppermute | solution.py:234
  145.4 3.8 %copy-start.7 = (s32[1,8]{1,0:T(1,128)S(1)}, s32[1,8]{1,0:T(1,128)}, u32[]{:S(2)}) copy-start(s32[1,8]{1,0:T(1,128)} %param.17) | copy-start | bytes 100
  145.4 19.0 %all-to-all-start.1 = ((bf16[8,64,1024]{2,1,0:T(8,128)(2,1)}), bf16[8,64,1024]{2,1,0:T(8,128)(2,1)S(1)}, u32[]{:S(2)}, u32[]{:S(2)}) async-start(bf16[8,64,1024]{2,1,0:T(8,128)(2,1)} %fusion.6), calls=%async_computation.1 | async-start | bytes 2097152 | tf_op jit(solution)/shard_map/all_to_all | solution.py:336

commit v4 on v3

--- a/solution.py
+++ b/solution.py
@@ -155,34 +155,49 @@
                 acc_out[h] = acc
 
 
-def shared_attend(q, state, blocks, tree=None):
+def shared_attend(q, state, blocks, tree=None, local=None):
     kv_heads, rows, _ = q.shape
+    whole = lambda a: pl.BlockSpec(a.shape, lambda i, f: (0,) * a.ndim)
+    blocks = tuple(blocks)
+    block_specs = [whole(b) for b in blocks]
+    group = jnp.zeros((1,), jnp.int32)
+    if local is not None:
+        cache, group = local
+        picked = pl.BlockSpec(
+            (cache.shape[0], None) + cache.shape[2:], lambda i, f: (0, f[1], 0, 0)
+        )
+        blocks = (cache,) + blocks
+        block_specs = [picked] + block_specs
     n_blocks = len(blocks)
-    whole = lambda a: pl.BlockSpec(a.shape, lambda i, f: (0,) * a.ndim)
-    ones = jnp.ones((blocks[0].shape[1], HD), jnp.bfloat16)
-    operands = (q,) + tuple(state) + tuple(blocks) + (ones,)
+    block_len = blocks[-1].shape[-2]
+    ones = jnp.ones((block_len, HD), jnp.bfloat16)
+    operands = (q,) + tuple(state) + blocks + (ones,)
+    specs = [whole(a) for a in (q,) + tuple(state)] + block_specs + [whole(ones)]
     if tree is not None:
         draft_kv, reach_rows, flag = tree
-        operands += (draft_kv, reach_rows, jnp.ones((draft_kv.shape[1], HD), jnp.bfloat16))
+        extra = (draft_kv, reach_rows, jnp.ones((draft_kv.shape[1], HD), jnp.bfloat16))
+        operands += extra
+        specs += [whole(a) for a in extra]
     else:
         flag = jnp.zeros((1,), jnp.int32)
-    keys = sum(b.shape[1] for b in blocks)
+    keys = block_len * n_blocks
+    scalars = jnp.concatenate([flag.reshape(1), group.reshape(1)]).astype(jnp.int32)
     return pl.pallas_call(
         functools.partial(shared_kernel, kv_heads, n_blocks, tree is not None),
         out_shape=tuple(jax.ShapeDtypeStruct(s.shape, s.dtype) for s in state),
         grid_spec=pltpu.PrefetchScalarGridSpec(
             num_scalar_prefetch=1,
             grid=(1,),
-            in_specs=[whole(a) for a in operands],
+            in_specs=specs,
             out_specs=[whole(s) for s in state],
         ),
         compiler_params=pltpu.CompilerParams(vmem_limit_bytes=48 * 1024 * 1024),
         cost_estimate=pl.CostEstimate(
             flops=6 * kv_heads * rows * keys * HD,
             transcendentals=kv_heads * rows * keys,
-            bytes_accessed=sum(b.size * 2 for b in blocks) + q.size * 2,
+            bytes_accessed=keys * blocks[-1].shape[-1] * 4 + q.size * 2,
         ),
-    )(flag, *operands)
+    )(scalars, *operands)
 
 
 def tree_reach(parent_row):
@@ -212,7 +227,7 @@
 
 
 def exchange_shared(shared_cache, group_ids, req_index, req_count, distances):
-    received = [pick_group(shared_cache, group_ids, req_index)]
+    received = []
     for k in distances:
         pairs = [(r, partner(r, k, req_count)) for r in range(req_count)]
         sent = pick_group(shared_cache, group_ids, partner(req_index, k, req_count))
@@ -286,8 +301,13 @@
     reach = tree_reach(parents[0])
     reach_rows = jnp.tile(reach.astype(jnp.float32), (QPK, 1))
     flag = (seq_index == 0).astype(jnp.int32).reshape(1)
-    state = shared_attend(queries, state, blocks[:2], (draft_kv[0], reach_rows, flag))
-    for blk in blocks[2:]:
+    own_group = jnp.sum(
+        jnp.where(jnp.arange(group_ids.shape[0], dtype=jnp.int32) == req_index, group_ids, 0)
+    )
+    state = shared_attend(
+        queries, state, blocks[:1], (draft_kv[0], reach_rows, flag), (shared_cache, own_group)
+    )
+    for blk in blocks[1:]:
         state = shared_attend(queries, state, [blk])
     m, l, acc = state
 

time: 166 us -> 166 us (level)
    unnamed x18 -> x16, local copies, waits for them, and re-layouts: 3.96 us -> 2.92 us
where the time goes in v4:
time: 166 us
  waiting for transfers between devices  70.1 us (42%)
  Pallas kernels  46.9 us (28%)
  starting transfers between devices  19.6 us (12%)
  matrix products  9.48 us (6%)
  other arithmetic  8.21 us (5%)
  local copies, waits for them, and re-layouts  7.83 us (5%)
  between operations  3.61 us (2%)
    ppermute x4, waiting for transfers between devices, exchange_to_owner(): received.append(lax.ppermute(piece, ('req', 'seq'), pairs))  43 us
    pallas_call x1, Pallas kernels, own_attend(): pl.pallas_call(functools.partial(own_kernel, kv_heads, block), out_shape=...  24.6 us
    pallas_call x3, Pallas kernels, shared_attend(): pl.pallas_call(functools.partial(shared_kernel, kv_heads, n_blocks, tree...  22.3 us
    all_to_all x1, waiting for transfers between devices, layer(): pieces = lax.all_to_all(product, out_group, 0, 0, tiled=True)  13.8 us
    ppermute x2, waiting for transfers between devices, exchange_shared(): received.append(lax.ppermute(sent, 'req', pairs))  13.3 us
    ppermute x4, starting transfers between devices, exchange_to_owner(): received.append(lax.ppermute(piece, ('req', 'seq'), pairs))  9.19 us
    dot_general x1, matrix products, layer(): jnp.einsum('ik,kcj->cij', attended, out_weight.reshape(out_weight.shape[0...  8.44 us
    all_to_all x1, starting transfers between devices, layer(): pieces = lax.all_to_all(product, out_group, 0, 0, tiled=True)  3.69 us
  transfers between devices with their start and end apart: 8, of which 6 were waited for; matrix products, arithmetic and copies ran while one was open for 4% of the time, Pallas kernels for 22%

profile of v4, /device:TPU:8, one launch (start us, length us, event | category | flops | bytes accessed | tf_op | source)
XLA Modules:
  0.0 165.8 jit_solution(2188780879872973051)
XLA Ops:
  0.6 1.4 fusion.27
  4.0 0.0 copy-start.4
  4.1 3.1 %bitcast_select_fusion = (bf16[2,1,512,512]{3,2,0,1:T(8,128)(2,1)S(1)}, bf16[2,512,512]{2,1,0:T(8,128)(2,1)}, bf16[2,512,512]{2,1,0:T(8,128)(2,1)}) fusion(pred[]{:T(512)S(6)} %eq.70, bf16[2,2,512,512]{3,2,1,0:T(8,128)(2,1)} %rest_0_.1, pred[]{:T(512)S(6)} %eq.67, pred[]{:T(512)S(6)} %eq.59), kind=kLoop, calls=%fused_computation.14 | loop fusion | flops 1572864 | bytes 5242883 | tf_op jit(solution)/shard_map/jit(_where)/select_n | solution.py:219
  7.2 0.0 collective-permute-start
  7.2 3.0 %collective-permute-start.1 = (bf16[2,512,512]{2,1,0:T(8,128)(2,1)}, bf16[2,512,512]{2,1,0:T(8,128)(2,1)}, u32[]{:S(2)}, u32[]{:S(2)}) collective-permute-start(bf16[2,512,512]{2,1,0:T(8,128)(2,1)} %get-tuple-element.33), channel_id=1, source_target_pairs={{0,8},{4,12},{8,0},{12,4},{1,9},{5,13},{9,1},{13,5},{2,10},{6,14},... | collective-permute-start | bytes 3145736 | tf_op jit(solution)/shard_map/ppermute | solution.py:234
  10.9 0.0 copy-done.4
  10.9 0.1 copy.35
  11.0 1.0 copy.18
  12.0 0.0 copy-done.5
  12.0 0.2 convolution_minimum_fusion.5
  12.2 0.2 convolution_minimum_fusion.4
  12.4 0.2 convolution_minimum_fusion.3
  12.5 0.2 convolution_minimum_fusion.2
  12.7 0.2 convolution_minimum_fusion.1
  12.9 0.2 fusion.10
  13.0 0.7 pad_add_fusion.flag_ref
  13.7 0.9 broadcast_in_dim.38.ones_ref
  14.6 24.6 %shard_map.104 = (f32[4,512,1]{2,1,0:T(8,128)}, f32[4,512,128]{2,1,0:T(8,128)}, f32[4,512,128]{2,1,0:T(8,128)}) custom-call(s32[1]{0:T(128)} %bitcast.6.nv_ref, bf16[4,512,128]{2,1,0:T(8,128)(2,1)} %bitcast.92, bf16[2,8192,512]{2,1,0:T(8,128)(2,1)} %bitcast.109, bf16[2048,128]{1,0:T(8,128)(2,1)} %broadcast_in_dim.38.ones_ref), custom_call_target="tpu_custom_call" | custom-call | flops 12884901888 | bytes 17301504 | tf_op jit(solution)/shard_map/pallas_call | solution.py:96
  39.2 13.3 %collective-permute-done.rest_1_ = bf16[2,512,512]{2,1,0:T(8,128)(2,1)} collective-permute-done((bf16[2,512,512]{2,1,0:T(8,128)(2,1)}, bf16[2,512,512]{2,1,0:T(8,128)(2,1)}, u32[]{:S(2)}, u32[]{:S(2)}) %collective-permute-start) | collective-permute-done | bytes 1048608 | tf_op jit(solution)/shard_map/ppermute | solution.py:234
  52.6 0.0 copy-done
  52.6 0.0 copy-done.3
  52.6 0.0 copy-start.2
  52.6 1.2 copy-done.2
  53.8 11.9 %shard_map.105 = (f32[4,512,1]{2,1,0:T(8,128)S(1)}, f32[4,512,128]{2,1,0:T(8,128)S(1)}, f32[4,512,128]{2,1,0:T(8,128)S(1)}) custom-call(s32[2]{0:T(128)S(1)} %pad_add_fusion.flag_ref, bf16[4,512,128]{2,1,0:T(8,128)(2,1)S(1)} %bitcast.93, f32[4,512,1]{2,1,0:T(8,128)S(1)} %copy-done.2, f32[4,512,128]{2,1,0:T(8,128)} %get-tuple-element.14.l_ref, ...), custom_call_target="tpu_custom_call" | custom-call | flops 1610612736 | bytes 2621440 | tf_op jit(solution)/shard_map/pallas_call | solution.py:185
  65.7 0.0 copy-start.1
  65.7 1.0 copy-done.1
  66.7 0.0 collective-permute-done.1.rest_0_
  66.7 6.3 %shard_map.106 = (f32[4,512,1]{2,1,0:T(8,128)S(1)}, f32[4,512,128]{2,1,0:T(8,128)S(1)}, f32[4,512,128]{2,1,0:T(8,128)S(1)}) custom-call(s32[2]{0:T(128)S(1)} %broadcast_11_flag_ref.2.flag_ref, bf16[4,512,128]{2,1,0:T(8,128)(2,1)S(1)} %bitcast.94, f32[4,512,1]{2,1,0:T(8,128)S(1)} %get-tuple-element.16.m_ref, f32[4,512,128]{2,1,0:T(8,128)S(1)} %get-tuple-element.17.l_ref, ...), custom_call_target="tpu_custom_call" | custom-call | flops 805306368 | bytes 1572864 | tf_op jit(solution)/shard_map/pallas_call | solution.py:185
  73.0 0.3 slice_reduce_fusion
  73.4 0.1 divide_convert_fusion
  73.5 0.3 reduce.2
  73.9 0.1 reshape_squeeze.10
  73.9 0.1 maximum_bitcast_fusion
  74.1 0.1 reshape_squeeze.11
  74.1 0.1 maximum_bitcast_fusion.1
  74.2 0.9 pad_maximum_fusion
  75.1 3.7 %all-to-all-start = ((bf16[32,66,128]{2,1,0:T(8,128)(2,1)}), bf16[32,66,128]{2,1,0:T(8,128)(2,1)S(1)}, u32[]{:S(2)}, u32[]{:S(2)}) async-start(bf16[32,66,128]{2,1,0:T(8,128)(2,1)} %pad_maximum_fusion), calls=%async_computation | async-start | bytes 1179648 | tf_op jit(solution)/shard_map/all_to_all | solution.py:323
  78.8 1.1 dynamic-slice_bitcast_fusion
  79.9 6.2 %collective-permute-start.2 = (bf16[2,512,128]{2,1,0:T(8,128)(2,1)}, bf16[2,512,128]{2,1,0:T(8,128)(2,1)S(1)}, u32[]{:S(2)}, u32[]{:S(2)}) collective-permute-start(bf16[2,512,128]{2,1,0:T(8,128)(2,1)} %get-tuple-element.38), channel_id=1, source_target_pairs={{0,12},{1,13},{2,14},{3,15},{4,8},{5,9},{6,10},{7,11},{8,4},{9,5},... | collective-permute-start | bytes 786440 | tf_op jit(solution)/shard_map/ppermute | solution.py:249
  86.1 0.0 collective-permute-start.3
  86.1 2.7 %collective-permute-start.4 = (bf16[2,512,128]{2,1,0:T(8,128)(2,1)}, bf16[2,512,128]{2,1,0:T(8,128)(2,1)S(1)}, u32[]{:S(2)}, u32[]{:S(2)}) collective-permute-start(bf16[2,512,128]{2,1,0:T(8,128)(2,1)} %get-tuple-element.36), channel_id=1, source_target_pairs={{0,14},{1,15},{2,12},{3,13},{4,10},{5,11},{6,8},{7,9},{8,6},{9,7},... | collective-permute-start | bytes 786440 | tf_op jit(solution)/shard_map/ppermute | solution.py:249
  88.8 0.3 collective-permute-start.5
  89.1 0.0 all-to-all-done
  89.1 0.1 fusion.31
  89.2 0.1 fusion.18
  89.4 0.2 reshape.154.m_ref
  89.6 0.1 broadcast_in_dim.40
  89.6 0.3 multiply_reduce_fusion
  90.0 25.5 %collective-permute-done.2.rest_0_ = bf16[2,512,128]{2,1,0:T(8,128)(2,1)S(1)} collective-permute-done((bf16[2,512,128]{2,1,0:T(8,128)(2,1)}, bf16[2,512,128]{2,1,0:T(8,128)(2,1)S(1)}, u32[]{:S(2)}, u32[]{:S(2)}) %collective-permute-start.2) | collective-permute-done | bytes 262176 | tf_op jit(solution)/shard_map/ppermute | solution.py:249
  115.5 5.6 %collective-permute-done.3.rest_1_ = bf16[2,512,128]{2,1,0:T(8,128)(2,1)S(1)} collective-permute-done((bf16[2,512,128]{2,1,0:T(8,128)(2,1)}, bf16[2,512,128]{2,1,0:T(8,128)(2,1)S(1)}, u32[]{:S(2)}, u32[]{:S(2)}) %collective-permute-start.3) | collective-permute-done | bytes 262176 | tf_op jit(solution)/shard_map/ppermute | solution.py:249
  121.1 6.4 %collective-permute-done.4.rest_2_ = bf16[2,512,128]{2,1,0:T(8,128)(2,1)S(1)} collective-permute-done((bf16[2,512,128]{2,1,0:T(8,128)(2,1)}, bf16[2,512,128]{2,1,0:T(8,128)(2,1)S(1)}, u32[]{:S(2)}, u32[]{:S(2)}) %collective-permute-start.4) | collective-permute-done | bytes 262176 | tf_op jit(solution)/shard_map/ppermute | solution.py:249
  127.5 5.5 %collective-permute-done.5.rest_3_ = bf16[2,512,128]{2,1,0:T(8,128)(2,1)S(1)} collective-permute-done((bf16[2,512,128]{2,1,0:T(8,128)(2,1)}, bf16[2,512,128]{2,1,0:T(8,128)(2,1)S(1)}, u32[]{:S(2)}, u32[]{:S(2)}) %collective-permute-start.5) | collective-permute-done | bytes 262176 | tf_op jit(solution)/shard_map/ppermute | solution.py:249
  133.0 0.1 broadcast_in_dim.41.l_ref
  133.1 4.1 %shard_map.107 = (f32[1,512,1]{2,1,0:T(8,128)}, f32[1,512,128]{2,1,0:T(8,128)S(1)}, f32[1,512,128]{2,1,0:T(8,128)S(1)}) custom-call(s32[2]{0:T(128)S(1)} %broadcast_11_flag_ref.2.flag_ref, bf16[1,512,128]{2,1,0:T(8,128)(2,1)S(1)} %constant_dynamic-slice_fusion.q_ref, f32[1,512,1]{2,1,0:T(8,128)S(1)} %reshape.154.m_ref, ...), custom_call_target="tpu_custom_call" | custom-call | flops 805306368 | bytes 1179648 | tf_op jit(solution)/shard_map/pallas_call | solution.py:185
  137.3 0.1 copy.26
  137.4 0.1 reshape.153
  137.5 8.4 %fusion.6 = bf16[8,64,1024]{2,1,0:T(8,128)(2,1)} fusion(bf16[64,1024,1]{1,0,2:T(8,128)(2,1)S(1)} %reshape.153, bf16[128,8,8,1024]{3,2,1,0:T(8,128)(2,1)} %bitcast.110), kind=kOutput, calls=%fused_computation.5 | convolution fusion | flops 1074266112 | bytes 17956864 | tf_op jit(solution)/shard_map/ik,kcj->cij/dot_general | solution.py:350
  145.9 3.7 %all-to-all-start.1 = ((bf16[8,64,1024]{2,1,0:T(8,128)(2,1)}), bf16[8,64,1024]{2,1,0:T(8,128)(2,1)S(1)}, u32[]{:S(2)}, u32[]{:S(2)}) async-start(bf16[8,64,1024]{2,1,0:T(8,128)(2,1)} %fusion.6), calls=%async_computation.1 | async-start | bytes 2097152 | tf_op jit(solution)/shard_map/all_to_all | solution.py:356
  149.6 0.1 copy.28
  149.8 0.6 gather_fusion
  150.4 0.1 broadcast_select_fusion
  150.5 0.6 copy.29
  151.1 13.8 %all-to-all-done.1 = bf16[8,64,1024]{2,1,0:T(8,128)(2,1)S(1)} async-done(((bf16[8,64,1024]{2,1,0:T(8,128)(2,1)}), bf16[8,64,1024]{2,1,0:T(8,128)(2,1)S(1)}, u32[]{:S(2)}, u32[]{:S(2)}) %all-to-all-start.1) | async-done | bytes 1048608 | tf_op jit(solution)/shard_map/all_to_all | solution.py:356
  164.9 0.8 reduce_sum.72
  (20 shorter events, 0.2 us)
Async XLA Ops:
  4.0 6.8 %copy-start.4 = (bf16[1,64,4096]{2,1,0:T(8,128)(2,1)S(1)}, bf16[1,64,4096]{2,1,0:T(8,128)(2,1)}, u32[]{:S(2)}) copy-start(bf16[1,64,4096]{2,1,0:T(8,128)(2,1)} %param.9) | copy-start | bytes 1572868
  7.2 4.8 %copy-start.5 = (s32[1,64]{1,0:T(1,128)S(1)}, s32[1,64]{1,0:T(1,128)}, u32[]{:S(2)}) copy-start(s32[1,64]{1,0:T(1,128)} %param.16) | copy-start | bytes 772
  7.2 45.4 %collective-permute-start = (bf16[2,512,512]{2,1,0:T(8,128)(2,1)}, bf16[2,512,512]{2,1,0:T(8,128)(2,1)}, u32[]{:S(2)}, u32[]{:S(2)}) collective-permute-start(bf16[2,512,512]{2,1,0:T(8,128)(2,1)} %get-tuple-element.34), channel_id=1, source_target_pairs={{0,4},{4,0},{8,12},{12,8},{1,5},{5,1},{9,13},{13,9},{2,6},{6,2},{1... | collective-permute-start | bytes 3145736 | tf_op jit(solution)/shard_map/ppermute | solution.py:234
  7.2 59.6 %collective-permute-start.1 = (bf16[2,512,512]{2,1,0:T(8,128)(2,1)}, bf16[2,512,512]{2,1,0:T(8,128)(2,1)}, u32[]{:S(2)}, u32[]{:S(2)}) collective-permute-start(bf16[2,512,512]{2,1,0:T(8,128)(2,1)} %get-tuple-element.33), channel_id=1, source_target_pairs={{0,8},{4,12},{8,0},{12,4},{1,9},{5,13},{9,1},{13,5},{2,10},{6,14},... | collective-permute-start | bytes 3145736 | tf_op jit(solution)/shard_map/ppermute | solution.py:234
  14.6 38.0 %copy-start = (bf16[64,4,8,128]{3,0,2,1:T(8,128)(2,1)S(1)}, bf16[64,4,8,128]{3,0,2,1:T(8,128)(2,1)}, u32[]{:S(2)}) copy-start(bf16[64,4,8,128]{3,0,2,1:T(8,128)(2,1)} %copy.18) | copy-start | bytes 1572868
  14.6 38.0 %copy-start.3 = (bf16[1,2,64,512]{3,2,1,0:T(8,128)(2,1)S(1)}, bf16[1,2,64,512]{3,2,1,0:T(8,128)(2,1)}, u32[]{:S(2)}) copy-start(bf16[1,2,64,512]{3,2,1,0:T(8,128)(2,1)} %param.10) | copy-start | bytes 393220
  52.6 1.2 copy-start.2
  65.7 1.0 copy-start.1
  75.1 14.0 %all-to-all-start = ((bf16[32,66,128]{2,1,0:T(8,128)(2,1)}), bf16[32,66,128]{2,1,0:T(8,128)(2,1)S(1)}, u32[]{:S(2)}, u32[]{:S(2)}) async-start(bf16[32,66,128]{2,1,0:T(8,128)(2,1)} %pad_maximum_fusion), calls=%async_computation | async-start | bytes 1179648 | tf_op jit(solution)/shard_map/all_to_all | solution.py:323
  79.9 35.6 %collective-permute-start.2 = (bf16[2,512,128]{2,1,0:T(8,128)(2,1)}, bf16[2,512,128]{2,1,0:T(8,128)(2,1)S(1)}, u32[]{:S(2)}, u32[]{:S(2)}) collective-permute-start(bf16[2,512,128]{2,1,0:T(8,128)(2,1)} %get-tuple-element.38), channel_id=1, source_target_pairs={{0,12},{1,13},{2,14},{3,15},{4,8},{5,9},{6,10},{7,11},{8,4},{9,5},... | collective-permute-start | bytes 786440 | tf_op jit(solution)/shard_map/ppermute | solution.py:249
  86.1 34.9 %collective-permute-start.3 = (bf16[2,512,128]{2,1,0:T(8,128)(2,1)}, bf16[2,512,128]{2,1,0:T(8,128)(2,1)S(1)}, u32[]{:S(2)}, u32[]{:S(2)}) collective-permute-start(bf16[2,512,128]{2,1,0:T(8,128)(2,1)} %get-tuple-element.37), channel_id=1, source_target_pairs={{0,13},{1,12},{2,15},{3,14},{4,9},{5,8},{6,11},{7,10},{8,5},{9,4},... | collective-permute-start | bytes 786440 | tf_op jit(solution)/shard_map/ppermute | solution.py:249
  86.1 41.3 %collective-permute-start.4 = (bf16[2,512,128]{2,1,0:T(8,128)(2,1)}, bf16[2,512,128]{2,1,0:T(8,128)(2,1)S(1)}, u32[]{:S(2)}, u32[]{:S(2)}) collective-permute-start(bf16[2,512,128]{2,1,0:T(8,128)(2,1)} %get-tuple-element.36), channel_id=1, source_target_pairs={{0,14},{1,15},{2,12},{3,13},{4,10},{5,11},{6,8},{7,9},{8,6},{9,7},... | collective-permute-start | bytes 786440 | tf_op jit(solution)/shard_map/ppermute | solution.py:249
  88.8 44.2 %collective-permute-start.5 = (bf16[2,512,128]{2,1,0:T(8,128)(2,1)}, bf16[2,512,128]{2,1,0:T(8,128)(2,1)S(1)}, u32[]{:S(2)}, u32[]{:S(2)}) collective-permute-start(bf16[2,512,128]{2,1,0:T(8,128)(2,1)} %get-tuple-element.35), channel_id=1, source_target_pairs={{0,15},{1,14},{2,13},{3,12},{4,11},{5,10},{6,9},{7,8},{8,7},{9,6},... | collective-permute-start | bytes 786440 | tf_op jit(solution)/shard_map/ppermute | solution.py:249
  145.9 3.8 %copy-start.6 = (s32[1,8]{1,0:T(1,128)S(1)}, s32[1,8]{1,0:T(1,128)}, u32[]{:S(2)}) copy-start(s32[1,8]{1,0:T(1,128)} %param.17) | copy-start | bytes 100
  145.9 19.0 %all-to-all-start.1 = ((bf16[8,64,1024]{2,1,0:T(8,128)(2,1)}), bf16[8,64,1024]{2,1,0:T(8,128)(2,1)S(1)}, u32[]{:S(2)}, u32[]{:S(2)}) async-start(bf16[8,64,1024]{2,1,0:T(8,128)(2,1)} %fusion.6), calls=%async_computation.1 | async-start | bytes 2097152 | tf_op jit(solution)/shard_map/all_to_all | solution.py:356

commit v5 on v4

--- a/solution.py
+++ b/solution.py
@@ -347,12 +347,8 @@
     out_group = ("tensor", "seq")
     owners = lax.axis_size("tensor") * seq_count
     columns = out_weight.shape[1] // owners
-    product = jnp.einsum(
-        "ik,kcj->cij",
-        attended,
-        out_weight.reshape(out_weight.shape[0], owners, columns),
-        preferred_element_type=jnp.float32,
-    ).astype(jnp.bfloat16)
+    product = jnp.dot(attended, out_weight, preferred_element_type=jnp.float32).astype(jnp.bfloat16)
+    product = product.reshape(draft_len, owners, columns).transpose(1, 0, 2)
     pieces = lax.all_to_all(product, out_group, 0, 0, tiled=True)
     verified = jnp.sum(pieces.astype(jnp.float32), axis=0).astype(jnp.bfloat16)[None]
     accepted_kv = jnp.take(draft_kv[0], accepted[0], axis=1)[None]

time: 166 us -> 169 us (1.018)
  local copies, waits for them, and re-layouts: 7.83 us -> 9.91 us
    unnamed x16 -> x18, local copies, waits for them, and re-layouts: 2.92 us -> 3.96 us
where the time goes in v5:
time: 169 us; the launch traced here: 168 us
  waiting for transfers between devices  70.1 us (41%)
  Pallas kernels  47 us (28%)
  starting transfers between devices  19.5 us (12%)
  local copies, waits for them, and re-layouts  9.91 us (6%)
  matrix products  9.83 us (6%)
  other arithmetic  8.15 us (5%)
  between operations  3.62 us (2%)
    ppermute x4, waiting for transfers between devices, exchange_to_owner(): received.append(lax.ppermute(piece, ('req', 'seq'), pairs))  43 us
    pallas_call x1, Pallas kernels, own_attend(): pl.pallas_call(functools.partial(own_kernel, kv_heads, block), out_shape=...  24.7 us
    pallas_call x3, Pallas kernels, shared_attend(): pl.pallas_call(functools.partial(shared_kernel, kv_heads, n_blocks, tree...  22.3 us
    all_to_all x1, waiting for transfers between devices, layer(): pieces = lax.all_to_all(product, out_group, 0, 0, tiled=True)  13.8 us
    ppermute x2, waiting for transfers between devices, exchange_shared(): received.append(lax.ppermute(sent, 'req', pairs))  13.3 us
    ppermute x4, starting transfers between devices, exchange_to_owner(): received.append(lax.ppermute(piece, ('req', 'seq'), pairs))  9.22 us
    dot_general x1, matrix products, layer(): jnp.dot(attended, out_weight, preferred_element_type=jnp.float32)  8.79 us
    unnamed x18, local copies, waits for them, and re-layouts  3.96 us
  transfers between devices with their start and end apart: 8, of which 6 were waited for; matrix products, arithmetic and copies ran while one was open for 4% of the time, Pallas kernels for 22%

profile of v5, /device:TPU:8, one launch (start us, length us, event | category | flops | bytes accessed | tf_op | source)
XLA Modules:
  0.0 168.0 jit_solution(11556003503266198007)
XLA Ops:
  0.6 1.4 fusion.20
  4.0 0.0 copy-start.5
  4.1 3.1 %bitcast_select_fusion = (bf16[2,1,512,512]{3,2,0,1:T(8,128)(2,1)S(1)}, bf16[2,512,512]{2,1,0:T(8,128)(2,1)}, bf16[2,512,512]{2,1,0:T(8,128)(2,1)}) fusion(pred[]{:T(512)S(6)} %eq.70, bf16[2,2,512,512]{3,2,1,0:T(8,128)(2,1)} %rest_0_.1, pred[]{:T(512)S(6)} %eq.67, pred[]{:T(512)S(6)} %eq.59), kind=kLoop, calls=%fused_computation.11 | loop fusion | flops 1572864 | bytes 5242883 | tf_op jit(solution)/shard_map/jit(_where)/select_n | solution.py:219
  7.2 0.0 collective-permute-start
  7.2 3.0 %collective-permute-start.1 = (bf16[2,512,512]{2,1,0:T(8,128)(2,1)}, bf16[2,512,512]{2,1,0:T(8,128)(2,1)S(1)}, u32[]{:S(2)}, u32[]{:S(2)}) collective-permute-start(bf16[2,512,512]{2,1,0:T(8,128)(2,1)} %get-tuple-element.35), channel_id=1, source_target_pairs={{0,8},{4,12},{8,0},{12,4},{1,9},{5,13},{9,1},{13,5},{2,10},{6,14},... | collective-permute-start | bytes 3145736 | tf_op jit(solution)/shard_map/ppermute | solution.py:234
  10.9 0.0 copy-done.5
  10.9 0.1 copy.44
  11.0 1.0 copy.27
  12.0 0.0 copy-done.6
  12.0 0.2 convolution_minimum_fusion.5
  12.2 0.2 convolution_minimum_fusion.4
  12.4 0.2 convolution_minimum_fusion.3
  12.6 0.2 convolution_minimum_fusion.2
  12.8 0.2 convolution_minimum_fusion.1
  12.9 0.2 fusion.1
  13.1 0.6 pad_add_fusion.flag_ref
  13.7 0.9 broadcast_in_dim.38.ones_ref
  14.6 24.7 %shard_map.104 = (f32[4,512,1]{2,1,0:T(8,128)}, f32[4,512,128]{2,1,0:T(8,128)}, f32[4,512,128]{2,1,0:T(8,128)}) custom-call(s32[1]{0:T(128)} %bitcast.6.nv_ref, bf16[4,512,128]{2,1,0:T(8,128)(2,1)} %bitcast.92, bf16[2,8192,512]{2,1,0:T(8,128)(2,1)} %bitcast.111, bf16[2048,128]{1,0:T(8,128)(2,1)} %broadcast_in_dim.38.ones_ref), custom_call_target="tpu_custom_call" | custom-call | flops 12884901888 | bytes 17301504 | tf_op jit(solution)/shard_map/pallas_call | solution.py:96
  39.3 13.3 %collective-permute-done.rest_1_ = bf16[2,512,512]{2,1,0:T(8,128)(2,1)} collective-permute-done((bf16[2,512,512]{2,1,0:T(8,128)(2,1)}, bf16[2,512,512]{2,1,0:T(8,128)(2,1)}, u32[]{:S(2)}, u32[]{:S(2)}) %collective-permute-start) | collective-permute-done | bytes 1048608 | tf_op jit(solution)/shard_map/ppermute | solution.py:234
  52.6 0.0 copy-done
  52.6 0.0 copy-done.3
  52.6 1.2 copy-done.2
  53.9 11.9 %shard_map.105 = (f32[4,512,1]{2,1,0:T(8,128)S(1)}, f32[4,512,128]{2,1,0:T(8,128)S(1)}, f32[4,512,128]{2,1,0:T(8,128)S(1)}) custom-call(s32[2]{0:T(128)S(1)} %pad_add_fusion.flag_ref, bf16[4,512,128]{2,1,0:T(8,128)(2,1)S(1)} %bitcast.93, f32[4,512,1]{2,1,0:T(8,128)S(1)} %copy-done.2, f32[4,512,128]{2,1,0:T(8,128)} %get-tuple-element.14.l_ref, ...), custom_call_target="tpu_custom_call" | custom-call | flops 1610612736 | bytes 2621440 | tf_op jit(solution)/shard_map/pallas_call | solution.py:185
  65.8 1.0 copy-done.1
  66.8 0.0 collective-permute-done.1.rest_0_
  66.8 1.0 copy-done.4
  67.8 6.3 %shard_map.106 = (f32[4,512,1]{2,1,0:T(8,128)S(1)}, f32[4,512,128]{2,1,0:T(8,128)S(1)}, f32[4,512,128]{2,1,0:T(8,128)S(1)}) custom-call(s32[2]{0:T(128)S(1)} %broadcast_11_flag_ref.2.flag_ref, bf16[4,512,128]{2,1,0:T(8,128)(2,1)S(1)} %bitcast.94, f32[4,512,1]{2,1,0:T(8,128)S(1)} %get-tuple-element.16.m_ref, f32[4,512,128]{2,1,0:T(8,128)S(1)} %get-tuple-element.17.l_ref, ...), custom_call_target="tpu_custom_call" | custom-call | flops 805306368 | bytes 1572864 | tf_op jit(solution)/shard_map/pallas_call | solution.py:185
  74.1 0.3 slice_reduce_fusion
  74.4 0.1 divide_convert_fusion
  74.6 0.3 reduce.2
  74.9 0.1 reshape_squeeze.10
  75.0 0.1 maximum_bitcast_fusion
  75.1 0.1 reshape_squeeze.11
  75.2 0.1 maximum_bitcast_fusion.1
  75.3 0.9 pad_maximum_fusion
  76.2 3.7 %all-to-all-start = ((bf16[32,66,128]{2,1,0:T(8,128)(2,1)}), bf16[32,66,128]{2,1,0:T(8,128)(2,1)S(1)}, u32[]{:S(2)}, u32[]{:S(2)}) async-start(bf16[32,66,128]{2,1,0:T(8,128)(2,1)} %pad_maximum_fusion), calls=%async_computation | async-start | bytes 1179648 | tf_op jit(solution)/shard_map/all_to_all | solution.py:323
  79.9 1.1 dynamic-slice_bitcast_fusion
  80.9 6.3 %collective-permute-start.2 = (bf16[2,512,128]{2,1,0:T(8,128)(2,1)}, bf16[2,512,128]{2,1,0:T(8,128)(2,1)S(1)}, u32[]{:S(2)}, u32[]{:S(2)}) collective-permute-start(bf16[2,512,128]{2,1,0:T(8,128)(2,1)} %get-tuple-element.40), channel_id=1, source_target_pairs={{0,12},{1,13},{2,14},{3,15},{4,8},{5,9},{6,10},{7,11},{8,4},{9,5},... | collective-permute-start | bytes 786440 | tf_op jit(solution)/shard_map/ppermute | solution.py:249
  87.2 0.0 collective-permute-start.3
  87.2 2.7 %collective-permute-start.4 = (bf16[2,512,128]{2,1,0:T(8,128)(2,1)}, bf16[2,512,128]{2,1,0:T(8,128)(2,1)S(1)}, u32[]{:S(2)}, u32[]{:S(2)}) collective-permute-start(bf16[2,512,128]{2,1,0:T(8,128)(2,1)} %get-tuple-element.38), channel_id=1, source_target_pairs={{0,14},{1,15},{2,12},{3,13},{4,10},{5,11},{6,8},{7,9},{8,6},{9,7},... | collective-permute-start | bytes 786440 | tf_op jit(solution)/shard_map/ppermute | solution.py:249
  89.9 0.3 collective-permute-start.5
  90.2 0.0 all-to-all-done
  90.2 0.1 fusion.24
  90.3 0.1 fusion.11
  90.4 0.2 reshape.153.m_ref
  90.6 0.1 broadcast_in_dim.40
  90.7 0.3 multiply_reduce_fusion
  91.0 25.5 %collective-permute-done.2.rest_0_ = bf16[2,512,128]{2,1,0:T(8,128)(2,1)S(1)} collective-permute-done((bf16[2,512,128]{2,1,0:T(8,128)(2,1)}, bf16[2,512,128]{2,1,0:T(8,128)(2,1)S(1)}, u32[]{:S(2)}, u32[]{:S(2)}) %collective-permute-start.2) | collective-permute-done | bytes 262176 | tf_op jit(solution)/shard_map/ppermute | solution.py:249
  116.5 5.6 %collective-permute-done.3.rest_1_ = bf16[2,512,128]{2,1,0:T(8,128)(2,1)S(1)} collective-permute-done((bf16[2,512,128]{2,1,0:T(8,128)(2,1)}, bf16[2,512,128]{2,1,0:T(8,128)(2,1)S(1)}, u32[]{:S(2)}, u32[]{:S(2)}) %collective-permute-start.3) | collective-permute-done | bytes 262176 | tf_op jit(solution)/shard_map/ppermute | solution.py:249
  122.1 6.4 %collective-permute-done.4.rest_2_ = bf16[2,512,128]{2,1,0:T(8,128)(2,1)S(1)} collective-permute-done((bf16[2,512,128]{2,1,0:T(8,128)(2,1)}, bf16[2,512,128]{2,1,0:T(8,128)(2,1)S(1)}, u32[]{:S(2)}, u32[]{:S(2)}) %collective-permute-start.4) | collective-permute-done | bytes 262176 | tf_op jit(solution)/shard_map/ppermute | solution.py:249
  128.5 5.5 %collective-permute-done.5.rest_3_ = bf16[2,512,128]{2,1,0:T(8,128)(2,1)S(1)} collective-permute-done((bf16[2,512,128]{2,1,0:T(8,128)(2,1)}, bf16[2,512,128]{2,1,0:T(8,128)(2,1)S(1)}, u32[]{:S(2)}, u32[]{:S(2)}) %collective-permute-start.5) | collective-permute-done | bytes 262176 | tf_op jit(solution)/shard_map/ppermute | solution.py:249
  134.0 0.1 broadcast_in_dim.41.l_ref
  134.2 4.2 %shard_map.107 = (f32[1,512,1]{2,1,0:T(8,128)}, f32[1,512,128]{2,1,0:T(8,128)S(1)}, f32[1,512,128]{2,1,0:T(8,128)S(1)}) custom-call(s32[2]{0:T(128)S(1)} %broadcast_11_flag_ref.2.flag_ref, bf16[1,512,128]{2,1,0:T(8,128)(2,1)S(1)} %constant_dynamic-slice_fusion.q_ref, f32[1,512,1]{2,1,0:T(8,128)S(1)} %reshape.153.m_ref, ...), custom_call_target="tpu_custom_call" | custom-call | flops 805306368 | bytes 1179648 | tf_op jit(solution)/shard_map/pallas_call | solution.py:185
  138.4 0.1 copy.35
  138.5 8.8 %convolution_convert_fusion = bf16[64,8192]{1,0:T(8,128)(2,1)S(1)} fusion(bf16[1024,8192]{1,0:T(8,128)(2,1)} %param.13, bf16[8,8,8,128]{3,2,1,0:T(8,128)(2,1)S(1)} %bitcast.106), kind=kOutput, calls=%fused_computation.1 | convolution fusion | flops 1074266112 | bytes 17956864 | tf_op jit(solution)/shard_map/dot_general | solution.py:350
  147.3 0.0 copy-start.7
  147.3 1.1 copy.57
  148.3 3.6 %all-to-all-start.1 = ((bf16[8,64,1024]{2,1,0:T(8,128)(2,1)}), bf16[8,64,1024]{2,1,0:T(8,128)(2,1)S(1)}, u32[]{:S(2)}, u32[]{:S(2)}) async-start(bf16[8,64,1024]{2,1,0:T(8,128)(2,1)} %bitcast.90), calls=%async_computation.1 | async-start | bytes 2097152 | tf_op jit(solution)/shard_map/all_to_all | solution.py:352
  151.9 0.1 copy.37
  152.1 0.6 gather_fusion
  152.7 0.1 broadcast_select_fusion
  152.8 0.6 copy.38
  153.4 13.8 %all-to-all-done.1 = bf16[8,64,1024]{2,1,0:T(8,128)(2,1)S(1)} async-done(((bf16[8,64,1024]{2,1,0:T(8,128)(2,1)}), bf16[8,64,1024]{2,1,0:T(8,128)(2,1)S(1)}, u32[]{:S(2)}, u32[]{:S(2)}) %all-to-all-start.1) | async-done | bytes 1048608 | tf_op jit(solution)/shard_map/all_to_all | solution.py:352
  167.2 0.8 reduce_sum.72
  (22 shorter events, 0.2 us)
Async XLA Ops:
  4.0 6.8 %copy-start.5 = (bf16[1,64,4096]{2,1,0:T(8,128)(2,1)S(1)}, bf16[1,64,4096]{2,1,0:T(8,128)(2,1)}, u32[]{:S(2)}) copy-start(bf16[1,64,4096]{2,1,0:T(8,128)(2,1)} %param.9) | copy-start | bytes 1572868
  7.2 4.8 %copy-start.6 = (s32[1,64]{1,0:T(1,128)S(1)}, s32[1,64]{1,0:T(1,128)}, u32[]{:S(2)}) copy-start(s32[1,64]{1,0:T(1,128)} %param.16) | copy-start | bytes 772
  7.2 45.4 %collective-permute-start = (bf16[2,512,512]{2,1,0:T(8,128)(2,1)}, bf16[2,512,512]{2,1,0:T(8,128)(2,1)}, u32[]{:S(2)}, u32[]{:S(2)}) collective-permute-start(bf16[2,512,512]{2,1,0:T(8,128)(2,1)} %get-tuple-element.36), channel_id=1, source_target_pairs={{0,4},{4,0},{8,12},{12,8},{1,5},{5,1},{9,13},{13,9},{2,6},{6,2},{1... | collective-permute-start | bytes 3145736 | tf_op jit(solution)/shard_map/ppermute | solution.py:234
  7.2 59.6 %collective-permute-start.1 = (bf16[2,512,512]{2,1,0:T(8,128)(2,1)}, bf16[2,512,512]{2,1,0:T(8,128)(2,1)S(1)}, u32[]{:S(2)}, u32[]{:S(2)}) collective-permute-start(bf16[2,512,512]{2,1,0:T(8,128)(2,1)} %get-tuple-element.35), channel_id=1, source_target_pairs={{0,8},{4,12},{8,0},{12,4},{1,9},{5,13},{9,1},{13,5},{2,10},{6,14},... | collective-permute-start | bytes 3145736 | tf_op jit(solution)/shard_map/ppermute | solution.py:234
  14.6 38.0 %copy-start = (bf16[64,4,8,128]{3,0,2,1:T(8,128)(2,1)S(1)}, bf16[64,4,8,128]{3,0,2,1:T(8,128)(2,1)}, u32[]{:S(2)}) copy-start(bf16[64,4,8,128]{3,0,2,1:T(8,128)(2,1)} %copy.27) | copy-start | bytes 1572868
  14.6 38.0 %copy-start.3 = (bf16[1,2,64,512]{3,2,1,0:T(8,128)(2,1)S(1)}, bf16[1,2,64,512]{3,2,1,0:T(8,128)(2,1)}, u32[]{:S(2)}) copy-start(bf16[1,2,64,512]{3,2,1,0:T(8,128)(2,1)} %param.10) | copy-start | bytes 393220
  52.6 1.2 copy-start.2
  65.7 1.0 copy-start.1
  66.8 1.0 copy-start.4
  76.2 14.0 %all-to-all-start = ((bf16[32,66,128]{2,1,0:T(8,128)(2,1)}), bf16[32,66,128]{2,1,0:T(8,128)(2,1)S(1)}, u32[]{:S(2)}, u32[]{:S(2)}) async-start(bf16[32,66,128]{2,1,0:T(8,128)(2,1)} %pad_maximum_fusion), calls=%async_computation | async-start | bytes 1179648 | tf_op jit(solution)/shard_map/all_to_all | solution.py:323
  80.9 35.6 %collective-permute-start.2 = (bf16[2,512,128]{2,1,0:T(8,128)(2,1)}, bf16[2,512,128]{2,1,0:T(8,128)(2,1)S(1)}, u32[]{:S(2)}, u32[]{:S(2)}) collective-permute-start(bf16[2,512,128]{2,1,0:T(8,128)(2,1)} %get-tuple-element.40), channel_id=1, source_target_pairs={{0,12},{1,13},{2,14},{3,15},{4,8},{5,9},{6,10},{7,11},{8,4},{9,5},... | collective-permute-start | bytes 786440 | tf_op jit(solution)/shard_map/ppermute | solution.py:249
  87.2 34.9 %collective-permute-start.3 = (bf16[2,512,128]{2,1,0:T(8,128)(2,1)}, bf16[2,512,128]{2,1,0:T(8,128)(2,1)S(1)}, u32[]{:S(2)}, u32[]{:S(2)}) collective-permute-start(bf16[2,512,128]{2,1,0:T(8,128)(2,1)} %get-tuple-element.39), channel_id=1, source_target_pairs={{0,13},{1,12},{2,15},{3,14},{4,9},{5,8},{6,11},{7,10},{8,5},{9,4},... | collective-permute-start | bytes 786440 | tf_op jit(solution)/shard_map/ppermute | solution.py:249
  87.2 41.3 %collective-permute-start.4 = (bf16[2,512,128]{2,1,0:T(8,128)(2,1)}, bf16[2,512,128]{2,1,0:T(8,128)(2,1)S(1)}, u32[]{:S(2)}, u32[]{:S(2)}) collective-permute-start(bf16[2,512,128]{2,1,0:T(8,128)(2,1)} %get-tuple-element.38), channel_id=1, source_target_pairs={{0,14},{1,15},{2,12},{3,13},{4,10},{5,11},{6,8},{7,9},{8,6},{9,7},... | collective-permute-start | bytes 786440 | tf_op jit(solution)/shard_map/ppermute | solution.py:249
  89.9 44.1 %collective-permute-start.5 = (bf16[2,512,128]{2,1,0:T(8,128)(2,1)}, bf16[2,512,128]{2,1,0:T(8,128)(2,1)S(1)}, u32[]{:S(2)}, u32[]{:S(2)}) collective-permute-start(bf16[2,512,128]{2,1,0:T(8,128)(2,1)} %get-tuple-element.37), channel_id=1, source_target_pairs={{0,15},{1,14},{2,13},{3,12},{4,11},{5,10},{6,9},{7,8},{8,7},{9,6},... | collective-permute-start | bytes 786440 | tf_op jit(solution)/shard_map/ppermute | solution.py:249
  147.3 4.8 %copy-start.7 = (s32[1,8]{1,0:T(1,128)S(1)}, s32[1,8]{1,0:T(1,128)}, u32[]{:S(2)}) copy-start(s32[1,8]{1,0:T(1,128)} %param.17) | copy-start | bytes 100
  148.3 18.9 %all-to-all-start.1 = ((bf16[8,64,1024]{2,1,0:T(8,128)(2,1)}), bf16[8,64,1024]{2,1,0:T(8,128)(2,1)S(1)}, u32[]{:S(2)}, u32[]{:S(2)}) async-start(bf16[8,64,1024]{2,1,0:T(8,128)(2,1)} %bitcast.90), calls=%async_computation.1 | async-start | bytes 2097152 | tf_op jit(solution)/shard_map/all_to_all | solution.py:352
